TPU v7x, 512 devices: a whole 4x4x16 slice. The times are simulated.
512 devices in a mesh: dp: 32 (over y, x, core), tensor: 16 (over z).
Axes of the slice: x: 4, y: 4, z: 16, core: 2. Of those that a mesh axis runs over, the one named last changes fastest.
Arguments:
- activations: bfloat16 [32768, 4096], P('dp', 'tensor'), may hold values from -40 to 40
- labels: int32 [32768], P('dp'), may hold values from 0 to 7, as said below
Outputs:
- covariance: float32 [4096, 4096], P('tensor', 'dp')
- cross_covariance: float32 [8, 4096], P(None, 'tensor')
Inputs may be any that keep to these rules, and one draw needn't show every extreme that they name: Every one of the 8 classes labels at least one token.
All inputs are finite; a program needn't handle non-finite values.
Results may differ from a plain program's by a relative error of at most 0.0003.
Values may be sent and summed in bfloat16 or wider, within the bound.
No kernel may reach another device: no remote copies, remote signals or barrier semaphores. Data moves between devices by JAX's collectives and lax.ppermute only.
A program may use at most 64 MiB of HBM per device.

v0:
```python
import jax
import jax.numpy as jnp
from jax import lax
from jax.sharding import PartitionSpec as P

D = 4096
CLASSES = 8
CHUNKS = 4
RS_BITS = (0, 1, 3, 2, 4)


def butterfly_sum(x, axis, n):
    k = 1
    while k < n:
        perm = [(i, i ^ k) for i in range(n)]
        x = x + lax.ppermute(x, axis, perm)
        k *= 2
    return x


def butterfly_scatter(x, axis, n, bits):
    me = lax.axis_index(axis)
    nb = len(bits)
    tail = x.shape[1:]
    x = x.reshape((2,) * nb + tail)
    left = list(range(nb))
    for b in bits:
        pos = left.index(nb - 1 - b)
        mine = me >> b & 1
        keep = lax.dynamic_index_in_dim(x, mine, pos, keepdims=False)
        send = lax.dynamic_index_in_dim(x, 1 - mine, pos, keepdims=False)
        perm = [(i, i ^ 1 << b) for i in range(n)]
        x = keep + lax.ppermute(send, axis, perm)
        left.pop(pos)
    return x


def body(activations, labels):
    tok_rows, slice_width = activations.shape
    n_dp = lax.axis_size("dp")
    n_t = lax.axis_size("tensor")
    assert n_dp == 1 << len(RS_BITS)
    token_total = tok_rows * n_dp
    col_width = D // n_dp
    halves = slice_width // col_width
    w = col_width // CHUNKS
    classes = jnp.arange(CLASSES, dtype=jnp.int32)
    matches = labels[None, :] == classes[:, None]
    onehot = matches.astype(jnp.bfloat16)
    local_counts = jnp.sum(matches.astype(jnp.float32), axis=1)
    own_local = jnp.dot(onehot, activations, preferred_element_type=jnp.float32)
    stats = jnp.concatenate(
        [own_local, jnp.broadcast_to(local_counts[:, None], (CLASSES, 128))], axis=1
    )
    stats = butterfly_sum(stats, "dp", n_dp)
    own_sums = stats[:, :slice_width]
    class_counts = stats[:, slice_width]
    own_t = activations.T.reshape(halves, col_width, tok_rows)
    parts = [own_t[:, k * w : (k + 1) * w, :].reshape(halves * w, tok_rows) for k in range(CHUNKS)]
    pieces = []
    colsums = []
    for k in range(CHUNKS):
        part = parts[k]
        g = lax.all_gather(part, "tensor", axis=0, tiled=True)
        prod = lax.dot_general(
            g, activations, (((1,), (0,)), ((), ())), preferred_element_type=jnp.float32
        ).reshape(n_dp, w, slice_width)
        colsums.append(jnp.sum(g.astype(jnp.float32), axis=1).reshape(n_dp, w))
        if k == CHUNKS - 1:
            colsum = jnp.concatenate(colsums, axis=1)
            extra = jnp.zeros((n_dp, 8, slice_width), jnp.float32)
            extra = extra.at[:, 0, :col_width].set(colsum)
            prod = jnp.concatenate([prod, extra], axis=1)
        if k + 1 < CHUNKS:
            parts[k + 1], prod = lax.optimization_barrier((parts[k + 1], prod))
        piece = butterfly_scatter(prod, "dp", n_dp, RS_BITS)
        if k + 2 < CHUNKS:
            parts[k + 2], piece = lax.optimization_barrier((parts[k + 2], piece))
        pieces.append(piece)
    mean_cols = pieces[-1][w, :col_width] / token_total
    gram_cols = jnp.concatenate(pieces[:-1] + [pieces[-1][:w]], axis=0)
    mean_rows = jnp.sum(own_sums, axis=0) / token_total
    covariance = gram_cols.T / token_total - mean_rows[:, None] * mean_cols[None, :]
    cross_covariance = (own_sums - class_counts[:, None] * mean_rows[None, :]) / token_total
    return (covariance, cross_covariance)


def solution(mesh):
    in_specs = (P("dp", "tensor"), P("dp"))
    out_specs = (P("tensor", "dp"), P(None, "tensor"))
    return jax.shard_map(body, mesh=mesh, in_specs=in_specs, out_specs=out_specs, check_vma=False)
```

profile of v0, /device:TPU:32, one launch (start us, length us, event | category | flops | bytes accessed | tf_op | source)
XLA Modules:
  0.0 359.2 jit_solution(11233232944824296545)
XLA Ops:
  7.2 1.3 copy.32
  8.5 0.8 fusion.11
  9.4 78.0 %all-gather.5.cloned.1.call-done = bf16[1024,1024]{1,0:T(8,128)(2,1)} async-done(((bf16[64,1024]{1,0:T(8,128)(2,1)}), bf16[1024,1024]{1,0:T(8,128)(2,1)}) %all-gather.5.cloned.1.call-update) | async-done | bytes 2097168 | tf_op jit(solution)/shard_map/all_gather | solution.py:64
  87.4 2.3 fusion.12
  89.9 1.9 collective-permute-start
  91.9 1.9 collective-permute-done
  93.8 3.4 collective-permute-start.1
  97.2 6.9 %collective-permute-done.1 = f32[2,2,2,32,256]{4,3,2,1,0:T(8,128)S(1)} collective-permute-done((f32[2,2,2,32,256]{4,3,2,1,0:T(8,128)S(1)}, f32[2,2,2,32,256]{4,3,2,1,0:T(8,128)S(1)}, u32[]{:S(2)}, u32[]{:S(2)}) %collective-permute-start.1) | collective-permute-done | bytes 262176 | tf_op jit(solution)/shard_map/ppermute | solution.py:33
  104.1 3.4 collective-permute-start.2
  107.5 3.5 collective-permute-done.2
  111.1 4.9 %collective-permute-start.3 = (f32[2,32,256]{2,1,0:T(8,128)S(1)}, f32[2,32,256]{2,1,0:T(8,128)S(1)}, u32[]{:S(2)}, u32[]{:S(2)}) collective-permute-start(f32[2,32,256]{2,1,0:T(8,128)S(1)} %dynamic-slice_bitcast_fusion.11), channel_id=1, source_target_pairs={{0,64},{16,80},{32,96},{48,112},{64,0},{80,16},{96,32},{112,48},{1... | collective-permute-start | bytes 196616 | tf_op jit(solution)/shard_map/ppermute | solution.py:33
  116.0 2.8 collective-permute-done.3
  118.7 4.9 %collective-permute-start.4 = (f32[32,256]{1,0:T(8,128)S(1)}, f32[32,256]{1,0:T(8,128)S(1)}, u32[]{:S(2)}, u32[]{:S(2)}) collective-permute-start(f32[32,256]{1,0:T(8,128)S(1)} %dynamic-slice_bitcast_fusion.15), channel_id=1, source_target_pairs={{0,256},{16,272},{32,288},{48,304},{64,320},{80,336},{96,352},{112... | collective-permute-start | bytes 98312 | tf_op jit(solution)/shard_map/ppermute | solution.py:33
  123.7 2.4 collective-permute-done.4
  126.1 33.2 %all-gather.7.cloned.1.call-done = bf16[1024,1024]{1,0:T(8,128)(2,1)} async-done(((bf16[64,1024]{1,0:T(8,128)(2,1)}), bf16[1024,1024]{1,0:T(8,128)(2,1)}) %all-gather.7.cloned.1.call-update) | async-done | bytes 2097168 | tf_op jit(solution)/shard_map/all_gather | solution.py:64
  159.3 2.3 fusion.13
  161.8 1.9 collective-permute-start.5
  163.8 1.9 collective-permute-done.5
  165.7 3.4 collective-permute-start.6
  169.1 6.8 %collective-permute-done.6 = f32[2,2,2,32,256]{4,3,2,1,0:T(8,128)S(1)} collective-permute-done((f32[2,2,2,32,256]{4,3,2,1,0:T(8,128)S(1)}, f32[2,2,2,32,256]{4,3,2,1,0:T(8,128)S(1)}, u32[]{:S(2)}, u32[]{:S(2)}) %collective-permute-start.6) | collective-permute-done | bytes 262176 | tf_op jit(solution)/shard_map/ppermute | solution.py:33
  176.0 3.5 collective-permute-start.7
  179.5 3.4 collective-permute-done.7
  183.0 4.9 %collective-permute-start.8 = (f32[2,32,256]{2,1,0:T(8,128)S(1)}, f32[2,32,256]{2,1,0:T(8,128)S(1)}, u32[]{:S(2)}, u32[]{:S(2)}) collective-permute-start(f32[2,32,256]{2,1,0:T(8,128)S(1)} %dynamic-slice_bitcast_fusion.10), channel_id=1, source_target_pairs={{0,64},{16,80},{32,96},{48,112},{64,0},{80,16},{96,32},{112,48},{1... | collective-permute-start | bytes 196616 | tf_op jit(solution)/shard_map/ppermute | solution.py:33
  187.9 2.8 collective-permute-done.8
  190.6 4.9 %collective-permute-start.9 = (f32[32,256]{1,0:T(8,128)S(1)}, f32[32,256]{1,0:T(8,128)S(1)}, u32[]{:S(2)}, u32[]{:S(2)}) collective-permute-start(f32[32,256]{1,0:T(8,128)S(1)} %dynamic-slice_bitcast_fusion.14), channel_id=1, source_target_pairs={{0,256},{16,272},{32,288},{48,304},{64,320},{80,336},{96,352},{112... | collective-permute-start | bytes 98312 | tf_op jit(solution)/shard_map/ppermute | solution.py:33
  195.6 2.4 collective-permute-done.9
  198.0 33.4 %all-gather.9.cloned.1.call-done = bf16[1024,1024]{1,0:T(8,128)(2,1)} async-done(((bf16[64,1024]{1,0:T(8,128)(2,1)}), bf16[1024,1024]{1,0:T(8,128)(2,1)}) %all-gather.9.cloned.1.call-update) | async-done | bytes 2097168 | tf_op jit(solution)/shard_map/all_gather | solution.py:64
  231.3 3.4 fusion.14
  235.1 2.0 collective-permute-start.20
  237.2 1.1 collective-permute-done.20
  238.3 3.4 collective-permute-start.21
  241.7 2.2 collective-permute-done.21
  243.9 4.9 %collective-permute-start.22 = (f32[8,384]{1,0:T(8,128)S(1)}, f32[8,384]{1,0:T(8,128)S(1)}, u32[]{:S(2)}, u32[]{:S(2)}) collective-permute-start(f32[8,384]{1,0:T(8,128)S(1)} %add.185), channel_id=1, source_target_pairs={{0,64},{16,80},{32,96},{48,112},{64,0},{80,16},{96,32},{112,48},{1... | collective-permute-start | bytes 36872 | tf_op jit(solution)/shard_map/ppermute | solution.py:16
  248.8 2.2 collective-permute-done.22
  251.0 3.4 collective-permute-start.23
  254.5 2.1 collective-permute-done.23
  256.6 4.9 %collective-permute-start.24 = (f32[8,384]{1,0:T(8,128)S(1)}, f32[8,384]{1,0:T(8,128)S(1)}, u32[]{:S(2)}, u32[]{:S(2)}) collective-permute-start(f32[8,384]{1,0:T(8,128)S(1)} %add.187), channel_id=1, source_target_pairs={{0,256},{16,272},{32,288},{48,304},{64,320},{80,336},{96,352},{112... | collective-permute-start | bytes 36872 | tf_op jit(solution)/shard_map/ppermute | solution.py:16
  261.5 2.2 collective-permute-done.24
  263.7 0.6 broadcast_multiply_fusion
  264.3 1.3 constant_dynamic-slice_fusion.1
  265.6 0.9 copy.63
  266.5 1.9 collective-permute-start.10
  268.8 1.9 convert_reduce_fusion.2
  270.8 1.9 convert_reduce_fusion.1
  272.9 1.1 fusion.2
  274.0 3.4 collective-permute-start.11
  277.4 27.1 %all-gather.11.cloned.1.call-done = bf16[1024,1024]{1,0:T(8,128)(2,1)} async-done(((bf16[64,1024]{1,0:T(8,128)(2,1)}), bf16[1024,1024]{1,0:T(8,128)(2,1)}) %all-gather.11.cloned.1.call-update) | async-done | bytes 2097168 | tf_op jit(solution)/shard_map/all_gather | solution.py:64
  304.5 2.1 convert_reduce_fusion
  306.8 0.7 fusion.15
  307.8 1.9 collective-permute-start.15
  309.8 0.7 subtract_multiply_fusion
  310.5 1.0 bitcast_add_fusion.2
  311.5 3.4 collective-permute-start.12
  315.0 3.4 collective-permute-start.16
  318.4 0.9 collective-permute-done.12
  319.3 4.9 %collective-permute-start.13 = (f32[2,32,256]{2,1,0:T(8,128)S(1)}, f32[2,32,256]{2,1,0:T(8,128)S(1)}, u32[]{:S(2)}, u32[]{:S(2)}) collective-permute-start(f32[2,32,256]{2,1,0:T(8,128)S(1)} %dynamic-slice_bitcast_fusion.9), channel_id=1, source_target_pairs={{0,64},{16,80},{32,96},{48,112},{64,0},{80,16},{96,32},{112,48},{1... | collective-permute-start | bytes 196616 | tf_op jit(solution)/shard_map/ppermute | solution.py:33
  324.2 3.2 collective-permute-done.16
  327.5 2.5 collective-permute-start.17
  330.2 4.6 %collective-permute-done.17 = f32[2,2,40,256]{3,2,1,0:T(8,128)S(1)} collective-permute-done((f32[2,2,40,256]{3,2,1,0:T(8,128)S(1)}, f32[2,2,40,256]{3,2,1,0:T(8,128)S(1)}, u32[]{:S(2)}, u32[]{:S(2)}) %collective-permute-start.17) | collective-permute-done | bytes 163872 | tf_op jit(solution)/shard_map/ppermute | solution.py:33
  334.8 4.9 %collective-permute-start.18 = (f32[2,40,256]{2,1,0:T(8,128)S(1)}, f32[2,40,256]{2,1,0:T(8,128)S(1)}, u32[]{:S(2)}, u32[]{:S(2)}) collective-permute-start(f32[2,40,256]{2,1,0:T(8,128)S(1)} %dynamic-slice_bitcast_fusion.8), channel_id=1, source_target_pairs={{0,64},{16,80},{32,96},{48,112},{64,0},{80,16},{96,32},{112,48},{1... | collective-permute-start | bytes 245768 | tf_op jit(solution)/shard_map/ppermute | solution.py:33
  339.7 4.6 %collective-permute-start.14 = (f32[32,256]{1,0:T(8,128)S(1)}, f32[32,256]{1,0:T(8,128)S(1)}, u32[]{:S(2)}, u32[]{:S(2)}) collective-permute-start(f32[32,256]{1,0:T(8,128)S(1)} %dynamic-slice_bitcast_fusion.13), channel_id=1, source_target_pairs={{0,256},{16,272},{32,288},{48,304},{64,320},{80,336},{96,352},{112... | collective-permute-start | bytes 98312 | tf_op jit(solution)/shard_map/ppermute | solution.py:33
  344.4 2.9 collective-permute-start.19
  347.4 4.5 %collective-permute-done.19 = f32[40,256]{1,0:T(8,128)S(1)} collective-permute-done((f32[40,256]{1,0:T(8,128)S(1)}, f32[40,256]{1,0:T(8,128)S(1)}, u32[]{:S(2)}, u32[]{:S(2)}) %collective-permute-start.19) | collective-permute-done | bytes 40992 | tf_op jit(solution)/shard_map/ppermute | solution.py:33
  351.9 0.8 copy.41
  (85 shorter events, 3.0 us)
Async XLA Ops:
  7.2 80.2 %copy-start.2 = (bf16[1024,256]{1,0:T(8,128)(2,1)S(1)}, bf16[1024,256]{1,0:T(8,128)(2,1)}, u32[]{:S(2)}) copy-start(bf16[1024,256]{1,0:T(8,128)(2,1)} %param.4) | copy-start | bytes 1572868
  7.2 80.2 %all-gather.5.cloned.1.call-start = ((), (), s32[]{:S(2)}) async-start(), calls=%async_computation | async-start | bytes 2228224 | tf_op jit(solution)/shard_map/all_gather | solution.py:64
  9.3 150.0 %all-gather.7.cloned.1.call-start = ((), (), s32[]{:S(2)}) async-start(), calls=%async_computation.1 | async-start | bytes 2228224 | tf_op jit(solution)/shard_map/all_gather | solution.py:64
  89.7 141.6 %all-gather.9.cloned.1.call-start = ((), (), s32[]{:S(2)}) async-start(), calls=%async_computation.2 | async-start | bytes 2228224 | tf_op jit(solution)/shard_map/all_gather | solution.py:64
  89.9 3.8 %collective-permute-start = (f32[2,2,2,2,32,256]{5,4,2,1,0,3:T(8,128)S(1)}, f32[2,2,2,2,32,256]{5,4,2,1,0,3:T(8,128)S(1)}, u32[]{:S(2)}, u32[]{:S(2)}) collective-permute-start(f32[2,2,2,2,32,256]{5,4,2,1,0,3:T(8,128)S(1)} %bitcast.128), channel_id=1, source_target_pairs={{0,16},{16,0},{32,48},{48,32},{64,80},{80,64},{96,112},{112,96},{1... | collective-permute-start | bytes 1572872 | tf_op jit(solution)/shard_map/ppermute | solution.py:33
  93.8 10.2 %collective-permute-start.1 = (f32[2,2,2,32,256]{4,3,2,1,0:T(8,128)S(1)}, f32[2,2,2,32,256]{4,3,2,1,0:T(8,128)S(1)}, u32[]{:S(2)}, u32[]{:S(2)}) collective-permute-start(f32[2,2,2,32,256]{4,3,2,1,0:T(8,128)S(1)} %dynamic-slice_bitcast_fusion.3), channel_id=1, source_target_pairs={{0,32},{16,48},{32,0},{48,16},{64,96},{80,112},{96,64},{112,80},{1... | collective-permute-start | bytes 786440 | tf_op jit(solution)/shard_map/ppermute | solution.py:33
  104.1 6.9 %collective-permute-start.2 = (f32[2,2,32,256]{3,2,1,0:T(8,128)S(1)}, f32[2,2,32,256]{3,2,1,0:T(8,128)S(1)}, u32[]{:S(2)}, u32[]{:S(2)}) collective-permute-start(f32[2,2,32,256]{3,2,1,0:T(8,128)S(1)} %dynamic-slice_bitcast_fusion.7), channel_id=1, source_target_pairs={{0,128},{16,144},{32,160},{48,176},{64,192},{80,208},{96,224},{112... | collective-permute-start | bytes 393224 | tf_op jit(solution)/shard_map/ppermute | solution.py:33
  111.1 7.7 %collective-permute-start.3 = (f32[2,32,256]{2,1,0:T(8,128)S(1)}, f32[2,32,256]{2,1,0:T(8,128)S(1)}, u32[]{:S(2)}, u32[]{:S(2)}) collective-permute-start(f32[2,32,256]{2,1,0:T(8,128)S(1)} %dynamic-slice_bitcast_fusion.11), channel_id=1, source_target_pairs={{0,64},{16,80},{32,96},{48,112},{64,0},{80,16},{96,32},{112,48},{1... | collective-permute-start | bytes 196616 | tf_op jit(solution)/shard_map/ppermute | solution.py:33
  118.7 7.3 %collective-permute-start.4 = (f32[32,256]{1,0:T(8,128)S(1)}, f32[32,256]{1,0:T(8,128)S(1)}, u32[]{:S(2)}, u32[]{:S(2)}) collective-permute-start(f32[32,256]{1,0:T(8,128)S(1)} %dynamic-slice_bitcast_fusion.15), channel_id=1, source_target_pairs={{0,256},{16,272},{32,288},{48,304},{64,320},{80,336},{96,352},{112... | collective-permute-start | bytes 98312 | tf_op jit(solution)/shard_map/ppermute | solution.py:33
  161.6 142.9 %all-gather.11.cloned.1.call-start = ((), (), s32[]{:S(2)}) async-start(), calls=%async_computation.3 | async-start | bytes 2228224 | tf_op jit(solution)/shard_map/all_gather | solution.py:64
  161.8 3.8 %collective-permute-start.5 = (f32[2,2,2,2,32,256]{5,4,2,1,0,3:T(8,128)S(1)}, f32[2,2,2,2,32,256]{5,4,2,1,0,3:T(8,128)S(1)}, u32[]{:S(2)}, u32[]{:S(2)}) collective-permute-start(f32[2,2,2,2,32,256]{5,4,2,1,0,3:T(8,128)S(1)} %bitcast.129), channel_id=1, source_target_pairs={{0,16},{16,0},{32,48},{48,32},{64,80},{80,64},{96,112},{112,96},{1... | collective-permute-start | bytes 1572872 | tf_op jit(solution)/shard_map/ppermute | solution.py:33
  165.7 10.2 %collective-permute-start.6 = (f32[2,2,2,32,256]{4,3,2,1,0:T(8,128)S(1)}, f32[2,2,2,32,256]{4,3,2,1,0:T(8,128)S(1)}, u32[]{:S(2)}, u32[]{:S(2)}) collective-permute-start(f32[2,2,2,32,256]{4,3,2,1,0:T(8,128)S(1)} %dynamic-slice_bitcast_fusion.2), channel_id=1, source_target_pairs={{0,32},{16,48},{32,0},{48,16},{64,96},{80,112},{96,64},{112,80},{1... | collective-permute-start | bytes 786440 | tf_op jit(solution)/shard_map/ppermute | solution.py:33
  176.0 6.9 %collective-permute-start.7 = (f32[2,2,32,256]{3,2,1,0:T(8,128)S(1)}, f32[2,2,32,256]{3,2,1,0:T(8,128)S(1)}, u32[]{:S(2)}, u32[]{:S(2)}) collective-permute-start(f32[2,2,32,256]{3,2,1,0:T(8,128)S(1)} %dynamic-slice_bitcast_fusion.6), channel_id=1, source_target_pairs={{0,128},{16,144},{32,160},{48,176},{64,192},{80,208},{96,224},{112... | collective-permute-start | bytes 393224 | tf_op jit(solution)/shard_map/ppermute | solution.py:33
  183.0 7.7 %collective-permute-start.8 = (f32[2,32,256]{2,1,0:T(8,128)S(1)}, f32[2,32,256]{2,1,0:T(8,128)S(1)}, u32[]{:S(2)}, u32[]{:S(2)}) collective-permute-start(f32[2,32,256]{2,1,0:T(8,128)S(1)} %dynamic-slice_bitcast_fusion.10), channel_id=1, source_target_pairs={{0,64},{16,80},{32,96},{48,112},{64,0},{80,16},{96,32},{112,48},{1... | collective-permute-start | bytes 196616 | tf_op jit(solution)/shard_map/ppermute | solution.py:33
  190.6 7.3 %collective-permute-start.9 = (f32[32,256]{1,0:T(8,128)S(1)}, f32[32,256]{1,0:T(8,128)S(1)}, u32[]{:S(2)}, u32[]{:S(2)}) collective-permute-start(f32[32,256]{1,0:T(8,128)S(1)} %dynamic-slice_bitcast_fusion.14), channel_id=1, source_target_pairs={{0,256},{16,272},{32,288},{48,304},{64,320},{80,336},{96,352},{112... | collective-permute-start | bytes 98312 | tf_op jit(solution)/shard_map/ppermute | solution.py:33
  198.0 36.8 %copy-start.3 = (s32[1024]{0:T(1024)S(1)}, s32[1024]{0:T(1024)}, u32[]{:S(2)}) copy-start(s32[1024]{0:T(1024)} %param.5) | copy-start | bytes 12292
  234.7 33.7 %copy-start = (bf16[1024,1024]{1,0:T(8,128)(2,1)S(1)}, bf16[1024,1024]{1,0:T(8,128)(2,1)}, u32[]{:S(2)}) copy-start(bf16[1024,1024]{1,0:T(8,128)(2,1)} %all-gather.5.cloned.1.call-done) | copy-start | bytes 6291460
  235.1 3.2 collective-permute-start.20
  238.3 5.6 %collective-permute-start.21 = (f32[8,384]{1,0:T(8,128)S(1)}, f32[8,384]{1,0:T(8,128)S(1)}, u32[]{:S(2)}, u32[]{:S(2)}) collective-permute-start(f32[8,384]{1,0:T(8,128)S(1)} %fusion.10), channel_id=1, source_target_pairs={{0,32},{16,48},{32,0},{48,16},{64,96},{80,112},{96,64},{112,80},{1... | collective-permute-start | bytes 36872 | tf_op jit(solution)/shard_map/ppermute | solution.py:16
  243.9 7.1 %collective-permute-start.22 = (f32[8,384]{1,0:T(8,128)S(1)}, f32[8,384]{1,0:T(8,128)S(1)}, u32[]{:S(2)}, u32[]{:S(2)}) collective-permute-start(f32[8,384]{1,0:T(8,128)S(1)} %add.185), channel_id=1, source_target_pairs={{0,64},{16,80},{32,96},{48,112},{64,0},{80,16},{96,32},{112,48},{1... | collective-permute-start | bytes 36872 | tf_op jit(solution)/shard_map/ppermute | solution.py:16
  251.0 5.6 %collective-permute-start.23 = (f32[8,384]{1,0:T(8,128)S(1)}, f32[8,384]{1,0:T(8,128)S(1)}, u32[]{:S(2)}, u32[]{:S(2)}) collective-permute-start(f32[8,384]{1,0:T(8,128)S(1)} %add.186), channel_id=1, source_target_pairs={{0,128},{16,144},{32,160},{48,176},{64,192},{80,208},{96,224},{112... | collective-permute-start | bytes 36872 | tf_op jit(solution)/shard_map/ppermute | solution.py:16
  256.6 7.1 %collective-permute-start.24 = (f32[8,384]{1,0:T(8,128)S(1)}, f32[8,384]{1,0:T(8,128)S(1)}, u32[]{:S(2)}, u32[]{:S(2)}) collective-permute-start(f32[8,384]{1,0:T(8,128)S(1)} %add.187), channel_id=1, source_target_pairs={{0,256},{16,272},{32,288},{48,304},{64,320},{80,336},{96,352},{112... | collective-permute-start | bytes 36872 | tf_op jit(solution)/shard_map/ppermute | solution.py:16
  266.5 6.4 %collective-permute-start.10 = (f32[2,2,2,2,32,256]{5,4,2,1,0,3:T(8,128)}, f32[2,2,2,2,32,256]{5,4,2,1,0,3:T(8,128)}, u32[]{:S(2)}, u32[]{:S(2)}) collective-permute-start(f32[2,2,2,2,32,256]{5,4,2,1,0,3:T(8,128)} %bitcast.117), channel_id=1, source_target_pairs={{0,16},{16,0},{32,48},{48,32},{64,80},{80,64},{96,112},{112,96},{1... | collective-permute-start | bytes 1572872 | tf_op jit(solution)/shard_map/ppermute | solution.py:33
  274.0 36.5 %collective-permute-start.11 = (f32[2,2,2,32,256]{4,3,2,1,0:T(8,128)S(1)}, f32[2,2,2,32,256]{4,3,2,1,0:T(8,128)}, u32[]{:S(2)}, u32[]{:S(2)}) collective-permute-start(f32[2,2,2,32,256]{4,3,2,1,0:T(8,128)S(1)} %dynamic-slice_bitcast_fusion.1), channel_id=1, source_target_pairs={{0,32},{16,48},{32,0},{48,16},{64,96},{80,112},{96,64},{112,80},{1... | collective-permute-start | bytes 786440 | tf_op jit(solution)/shard_map/ppermute | solution.py:33
  304.5 2.3 copy-start.1
  307.5 2.3 copy-start.4
  307.8 7.1 %collective-permute-start.15 = (f32[2,2,2,2,40,256]{5,4,2,1,0,3:T(8,128)S(1)}, f32[2,2,2,2,40,256]{5,4,2,1,0,3:T(8,128)S(1)}, u32[]{:S(2)}, u32[]{:S(2)}) collective-permute-start(f32[2,2,2,2,40,256]{5,4,2,1,0,3:T(8,128)S(1)} %bitcast.127), channel_id=1, source_target_pairs={{0,16},{16,0},{32,48},{48,32},{64,80},{80,64},{96,112},{112,96},{1... | collective-permute-start | bytes 1966088 | tf_op jit(solution)/shard_map/ppermute | solution.py:33
  311.5 7.8 %collective-permute-start.12 = (f32[2,2,32,256]{3,2,1,0:T(8,128)S(1)}, f32[2,2,32,256]{3,2,1,0:T(8,128)S(1)}, u32[]{:S(2)}, u32[]{:S(2)}) collective-permute-start(f32[2,2,32,256]{3,2,1,0:T(8,128)S(1)} %dynamic-slice_bitcast_fusion.5), channel_id=1, source_target_pairs={{0,128},{16,144},{32,160},{48,176},{64,192},{80,208},{96,224},{112... | collective-permute-start | bytes 393224 | tf_op jit(solution)/shard_map/ppermute | solution.py:33
  315.0 12.4 %collective-permute-start.16 = (f32[2,2,2,40,256]{4,3,2,1,0:T(8,128)S(1)}, f32[2,2,2,40,256]{4,3,2,1,0:T(8,128)S(1)}, u32[]{:S(2)}, u32[]{:S(2)}) collective-permute-start(f32[2,2,2,40,256]{4,3,2,1,0:T(8,128)S(1)} %dynamic-slice_bitcast_fusion), channel_id=1, source_target_pairs={{0,32},{16,48},{32,0},{48,16},{64,96},{80,112},{96,64},{112,80},{1... | collective-permute-start | bytes 983048 | tf_op jit(solution)/shard_map/ppermute | solution.py:33
  319.3 10.8 %collective-permute-start.13 = (f32[2,32,256]{2,1,0:T(8,128)S(1)}, f32[2,32,256]{2,1,0:T(8,128)S(1)}, u32[]{:S(2)}, u32[]{:S(2)}) collective-permute-start(f32[2,32,256]{2,1,0:T(8,128)S(1)} %dynamic-slice_bitcast_fusion.9), channel_id=1, source_target_pairs={{0,64},{16,80},{32,96},{48,112},{64,0},{80,16},{96,32},{112,48},{1... | collective-permute-start | bytes 196616 | tf_op jit(solution)/shard_map/ppermute | solution.py:33
  327.5 7.2 %collective-permute-start.17 = (f32[2,2,40,256]{3,2,1,0:T(8,128)S(1)}, f32[2,2,40,256]{3,2,1,0:T(8,128)S(1)}, u32[]{:S(2)}, u32[]{:S(2)}) collective-permute-start(f32[2,2,40,256]{3,2,1,0:T(8,128)S(1)} %dynamic-slice_bitcast_fusion.4), channel_id=1, source_target_pairs={{0,128},{16,144},{32,160},{48,176},{64,192},{80,208},{96,224},{112... | collective-permute-start | bytes 491528 | tf_op jit(solution)/shard_map/ppermute | solution.py:33
  334.8 9.6 %collective-permute-start.18 = (f32[2,40,256]{2,1,0:T(8,128)S(1)}, f32[2,40,256]{2,1,0:T(8,128)S(1)}, u32[]{:S(2)}, u32[]{:S(2)}) collective-permute-start(f32[2,40,256]{2,1,0:T(8,128)S(1)} %dynamic-slice_bitcast_fusion.8), channel_id=1, source_target_pairs={{0,64},{16,80},{32,96},{48,112},{64,0},{80,16},{96,32},{112,48},{1... | collective-permute-start | bytes 245768 | tf_op jit(solution)/shard_map/ppermute | solution.py:33
  339.7 7.6 %collective-permute-start.14 = (f32[32,256]{1,0:T(8,128)S(1)}, f32[32,256]{1,0:T(8,128)S(1)}, u32[]{:S(2)}, u32[]{:S(2)}) collective-permute-start(f32[32,256]{1,0:T(8,128)S(1)} %dynamic-slice_bitcast_fusion.13), channel_id=1, source_target_pairs={{0,256},{16,272},{32,288},{48,304},{64,320},{80,336},{96,352},{112... | collective-permute-start | bytes 98312 | tf_op jit(solution)/shard_map/ppermute | solution.py:33
  344.4 7.4 %collective-permute-start.19 = (f32[40,256]{1,0:T(8,128)S(1)}, f32[40,256]{1,0:T(8,128)S(1)}, u32[]{:S(2)}, u32[]{:S(2)}) collective-permute-start(f32[40,256]{1,0:T(8,128)S(1)} %dynamic-slice_bitcast_fusion.12), channel_id=1, source_target_pairs={{0,256},{16,272},{32,288},{48,304},{64,320},{80,336},{96,352},{112... | collective-permute-start | bytes 122888 | tf_op jit(solution)/shard_map/ppermute | solution.py:33
Sparse Core Ops, SparseCore 0:
  10.6 76.6 all-gather.4
  89.8 69.4 all-gather.6
  161.8 69.5 all-gather.8
  234.9 69.6 all-gather.10
where the time goes:
time: 360 us; the launch traced here: 359 us
  waiting for transfers between devices  229 us (64%)
  starting transfers between devices  89.7 us (25%)
  between operations  14.4 us (4%)
  other arithmetic  10.6 us (3%)
  matrix products  8.88 us (2%)
  local copies, waits for them, and re-layouts  6.2 us (2%)
    all_gather x4, waiting for transfers between devices, body(): g = lax.all_gather(part, 'tensor', axis=0, tiled=True)  172 us
    ppermute x20, starting transfers between devices, butterfly_scatter(): x = keep + lax.ppermute(send, axis, perm)  70.9 us
    ppermute x20, waiting for transfers between devices, butterfly_scatter(): x = keep + lax.ppermute(send, axis, perm)  47.8 us
    ppermute x5, starting transfers between devices, butterfly_sum(): x = x + lax.ppermute(x, axis, perm)  18.6 us
    ppermute x5, waiting for transfers between devices, butterfly_sum(): x = x + lax.ppermute(x, axis, perm)  9.86 us
    dot_general x4, matrix products, body(): lax.dot_general(g, activations, (((1,), (0,)), ((), ())), preferred_eleme...  8.7 us
  transfers between devices with their start and end apart: 29, of which 24 were waited for; matrix products, arithmetic and copies ran while one was open for 4% of the time, Pallas kernels for 0%

commit v1 on v0

--- a/solution.py
+++ b/solution.py
@@ -7,6 +7,22 @@
 CLASSES = 8
 CHUNKS = 4
 RS_BITS = (0, 1, 3, 2, 4)
+
+
+def ring_gather(x, axis, dim):
+    ways, here, turn = (lax.axis_size(axis), lax.axis_index(axis), x.shape[dim])
+    shape = [n * ways if d == dim else n for d, n in enumerate(x.shape)]
+    full = lax.dynamic_update_slice_in_dim(jnp.zeros(shape, x.dtype), x, here * turn, axis=dim)
+    going_up = going_down = x
+    for far in range(1, ways // 2 + 1):
+        going_up = lax.ppermute(going_up, axis, [(d, (d + 1) % ways) for d in range(ways)])
+        full = lax.dynamic_update_slice_in_dim(full, going_up, (here - far) % ways * turn, axis=dim)
+        if 2 * far < ways:
+            going_down = lax.ppermute(going_down, axis, [(d, (d - 1) % ways) for d in range(ways)])
+            full = lax.dynamic_update_slice_in_dim(
+                full, going_down, (here + far) % ways * turn, axis=dim
+            )
+    return full
 
 
 def butterfly_sum(x, axis, n):
@@ -61,7 +77,7 @@
     colsums = []
     for k in range(CHUNKS):
         part = parts[k]
-        g = lax.all_gather(part, "tensor", axis=0, tiled=True)
+        g = ring_gather(part, "tensor", 0)
         prod = lax.dot_general(
             g, activations, (((1,), (0,)), ((), ())), preferred_element_type=jnp.float32
         ).reshape(n_dp, w, slice_width)

time: 360 us -> 374 us (1.039)
  the two profiles are of different devices: /device:TPU:32 before, /device:TPU:6 now
where the time goes in v1:
time: 374 us; the launch traced here: 371 us
  starting transfers between devices  297 us (79%)
  waiting for transfers between devices  58.6 us (16%)
  local copies, waits for them, and re-layouts  5.32 us (1%)
  matrix products  4.09 us (1%)
  other arithmetic  3.84 us (1%)
    ppermute x28, starting transfers between devices, ring_gather(): lax.ppermute(going_down, axis, [(d, (d - 1) % ways) for d in range(ways)])  146 us
    ppermute x20, starting transfers between devices, butterfly_scatter(): x = keep + lax.ppermute(send, axis, perm)  68.6 us
    ppermute x32, starting transfers between devices, ring_gather(): lax.ppermute(going_up, axis, [(d, (d + 1) % ways) for d in range(ways)])  61.3 us
    ppermute x32, waiting for transfers between devices, ring_gather(): lax.ppermute(going_up, axis, [(d, (d + 1) % ways) for d in range(ways)])  33 us
    ppermute x5, starting transfers between devices, butterfly_sum(): x = x + lax.ppermute(x, axis, perm)  20.4 us
    ppermute x20, waiting for transfers between devices, butterfly_scatter(): x = keep + lax.ppermute(send, axis, perm)  19.3 us
  transfers between devices with their start and end apart: 85, of which 32 were waited for; matrix products, arithmetic and copies ran while one was open for 2% of the time, Pallas kernels for 0%

profile of v1, /device:TPU:6, one launch (start us, length us, event | category | flops | bytes accessed | tf_op | source)
XLA Modules:
  0.0 371.5 jit_solution(13238996494468286477)
XLA Ops:
  5.8 2.7 collective-permute-start.81
  11.4 7.2 %collective-permute-start.82 = (f32[8,384]{1,0:T(8,128)S(1)}, f32[8,384]{1,0:T(8,128)S(1)}, u32[]{:S(2)}, u32[]{:S(2)}) collective-permute-start(f32[8,384]{1,0:T(8,128)S(1)} %add.460), channel_id=1, source_target_pairs={{0,64},{16,80},{32,96},{48,112},{64,0},{80,16},{96,32},{112,48},{1... | collective-permute-start | bytes 36872 | tf_op jit(solution)/shard_map/ppermute | solution.py:32
  18.6 1.9 collective-permute-start
  20.6 7.5 %collective-permute-start.1 = (bf16[64,1024]{1,0:T(8,128)(2,1)S(1)}, bf16[64,1024]{1,0:T(8,128)(2,1)S(1)}, u32[]{:S(2)}, u32[]{:S(2)}) collective-permute-start(bf16[64,1024]{1,0:T(8,128)(2,1)S(1)} %bitcast.141), channel_id=1, source_target_pairs={{0,15},{1,0},{2,1},{3,2},{4,3},{5,4},{6,5},{7,6},{8,7},{9,8},{10,9... | collective-permute-start | bytes 393224 | tf_op jit(solution)/shard_map/ppermute | solution.py:21
  28.1 3.5 collective-permute-start.83
  33.7 5.1 %collective-permute-start.84 = (f32[8,384]{1,0:T(8,128)S(1)}, f32[8,384]{1,0:T(8,128)S(1)}, u32[]{:S(2)}, u32[]{:S(2)}) collective-permute-start(f32[8,384]{1,0:T(8,128)S(1)} %add.462), channel_id=1, source_target_pairs={{0,256},{16,272},{32,288},{48,304},{64,320},{80,336},{96,352},{112... | collective-permute-start | bytes 36872 | tf_op jit(solution)/shard_map/ppermute | solution.py:32
  40.8 1.9 collective-permute-start.2
  42.8 5.1 %collective-permute-start.3 = (bf16[64,1024]{1,0:T(8,128)(2,1)S(1)}, bf16[64,1024]{1,0:T(8,128)(2,1)S(1)}, u32[]{:S(2)}, u32[]{:S(2)}) collective-permute-start(bf16[64,1024]{1,0:T(8,128)(2,1)S(1)} %collective-permute-done.1), channel_id=1, source_target_pairs={{0,15},{1,0},{2,1},{3,2},{4,3},{5,4},{6,5},{7,6},{8,7},{9,8},{10,9... | collective-permute-start | bytes 393224 | tf_op jit(solution)/shard_map/ppermute | solution.py:21
  50.8 5.1 %collective-permute-start.5 = (bf16[64,1024]{1,0:T(8,128)(2,1)S(1)}, bf16[64,1024]{1,0:T(8,128)(2,1)S(1)}, u32[]{:S(2)}, u32[]{:S(2)}) collective-permute-start(bf16[64,1024]{1,0:T(8,128)(2,1)S(1)} %collective-permute-done.3), channel_id=1, source_target_pairs={{0,15},{1,0},{2,1},{3,2},{4,3},{5,4},{6,5},{7,6},{8,7},{9,8},{10,9... | collective-permute-start | bytes 393224 | tf_op jit(solution)/shard_map/ppermute | solution.py:21
  59.4 5.4 %collective-permute-start.7 = (bf16[64,1024]{1,0:T(8,128)(2,1)S(1)}, bf16[64,1024]{1,0:T(8,128)(2,1)S(1)}, u32[]{:S(2)}, u32[]{:S(2)}) collective-permute-start(bf16[64,1024]{1,0:T(8,128)(2,1)S(1)} %collective-permute-done.5), channel_id=1, source_target_pairs={{0,15},{1,0},{2,1},{3,2},{4,3},{5,4},{6,5},{7,6},{8,7},{9,8},{10,9... | collective-permute-start | bytes 393224 | tf_op jit(solution)/shard_map/ppermute | solution.py:21
  68.6 5.1 %collective-permute-start.9 = (bf16[64,1024]{1,0:T(8,128)(2,1)S(1)}, bf16[64,1024]{1,0:T(8,128)(2,1)S(1)}, u32[]{:S(2)}, u32[]{:S(2)}) collective-permute-start(bf16[64,1024]{1,0:T(8,128)(2,1)S(1)} %collective-permute-done.7), channel_id=1, source_target_pairs={{0,15},{1,0},{2,1},{3,2},{4,3},{5,4},{6,5},{7,6},{8,7},{9,8},{10,9... | collective-permute-start | bytes 393224 | tf_op jit(solution)/shard_map/ppermute | solution.py:21
  77.0 5.1 %collective-permute-start.11 = (bf16[64,1024]{1,0:T(8,128)(2,1)S(1)}, bf16[64,1024]{1,0:T(8,128)(2,1)S(1)}, u32[]{:S(2)}, u32[]{:S(2)}) collective-permute-start(bf16[64,1024]{1,0:T(8,128)(2,1)S(1)} %collective-permute-done.9), channel_id=1, source_target_pairs={{0,15},{1,0},{2,1},{3,2},{4,3},{5,4},{6,5},{7,6},{8,7},{9,8},{10,9... | collective-permute-start | bytes 393224 | tf_op jit(solution)/shard_map/ppermute | solution.py:21
  85.1 5.1 %collective-permute-start.13 = (bf16[64,1024]{1,0:T(8,128)(2,1)S(1)}, bf16[64,1024]{1,0:T(8,128)(2,1)S(1)}, u32[]{:S(2)}, u32[]{:S(2)}) collective-permute-start(bf16[64,1024]{1,0:T(8,128)(2,1)S(1)} %collective-permute-done.11), channel_id=1, source_target_pairs={{0,15},{1,0},{2,1},{3,2},{4,3},{5,4},{6,5},{7,6},{8,7},{9,8},{10,9... | collective-permute-start | bytes 393224 | tf_op jit(solution)/shard_map/ppermute | solution.py:21
  93.2 6.1 %collective-permute-done.14 = bf16[64,1024]{1,0:T(8,128)(2,1)S(1)} collective-permute-done((bf16[64,1024]{1,0:T(8,128)(2,1)S(1)}, bf16[64,1024]{1,0:T(8,128)(2,1)S(1)}, u32[]{:S(2)}, u32[]{:S(2)}) %collective-permute-start.14) | collective-permute-done | bytes 131104 | tf_op jit(solution)/shard_map/ppermute | solution.py:18
  100.0 1.9 collective-permute-start.20
  102.0 5.1 %collective-permute-start.21 = (bf16[64,1024]{1,0:T(8,128)(2,1)S(1)}, bf16[64,1024]{1,0:T(8,128)(2,1)S(1)}, u32[]{:S(2)}, u32[]{:S(2)}) collective-permute-start(bf16[64,1024]{1,0:T(8,128)(2,1)S(1)} %bitcast.138), channel_id=1, source_target_pairs={{0,15},{1,0},{2,1},{3,2},{4,3},{5,4},{6,5},{7,6},{8,7},{9,8},{10,9... | collective-permute-start | bytes 393224 | tf_op jit(solution)/shard_map/ppermute | solution.py:21
  107.6 1.9 collective-permute-start.15
  109.9 1.9 collective-permute-start.22
  111.8 5.1 %collective-permute-start.23 = (bf16[64,1024]{1,0:T(8,128)(2,1)S(1)}, bf16[64,1024]{1,0:T(8,128)(2,1)S(1)}, u32[]{:S(2)}, u32[]{:S(2)}) collective-permute-start(bf16[64,1024]{1,0:T(8,128)(2,1)S(1)} %collective-permute-done.21), channel_id=1, source_target_pairs={{0,15},{1,0},{2,1},{3,2},{4,3},{5,4},{6,5},{7,6},{8,7},{9,8},{10,9... | collective-permute-start | bytes 393224 | tf_op jit(solution)/shard_map/ppermute | solution.py:21
  120.8 5.1 %collective-permute-start.25 = (bf16[64,1024]{1,0:T(8,128)(2,1)S(1)}, bf16[64,1024]{1,0:T(8,128)(2,1)S(1)}, u32[]{:S(2)}, u32[]{:S(2)}) collective-permute-start(bf16[64,1024]{1,0:T(8,128)(2,1)S(1)} %collective-permute-done.23), channel_id=1, source_target_pairs={{0,15},{1,0},{2,1},{3,2},{4,3},{5,4},{6,5},{7,6},{8,7},{9,8},{10,9... | collective-permute-start | bytes 393224 | tf_op jit(solution)/shard_map/ppermute | solution.py:21
  128.9 5.1 %collective-permute-start.27 = (bf16[64,1024]{1,0:T(8,128)(2,1)S(1)}, bf16[64,1024]{1,0:T(8,128)(2,1)S(1)}, u32[]{:S(2)}, u32[]{:S(2)}) collective-permute-start(bf16[64,1024]{1,0:T(8,128)(2,1)S(1)} %collective-permute-done.25), channel_id=1, source_target_pairs={{0,15},{1,0},{2,1},{3,2},{4,3},{5,4},{6,5},{7,6},{8,7},{9,8},{10,9... | collective-permute-start | bytes 393224 | tf_op jit(solution)/shard_map/ppermute | solution.py:21
  137.0 5.1 %collective-permute-start.29 = (bf16[64,1024]{1,0:T(8,128)(2,1)S(1)}, bf16[64,1024]{1,0:T(8,128)(2,1)S(1)}, u32[]{:S(2)}, u32[]{:S(2)}) collective-permute-start(bf16[64,1024]{1,0:T(8,128)(2,1)S(1)} %collective-permute-done.27), channel_id=1, source_target_pairs={{0,15},{1,0},{2,1},{3,2},{4,3},{5,4},{6,5},{7,6},{8,7},{9,8},{10,9... | collective-permute-start | bytes 393224 | tf_op jit(solution)/shard_map/ppermute | solution.py:21
  142.3 1.9 collective-permute-start.16
  146.2 5.1 %collective-permute-start.31 = (bf16[64,1024]{1,0:T(8,128)(2,1)S(1)}, bf16[64,1024]{1,0:T(8,128)(2,1)S(1)}, u32[]{:S(2)}, u32[]{:S(2)}) collective-permute-start(bf16[64,1024]{1,0:T(8,128)(2,1)S(1)} %collective-permute-done.29), channel_id=1, source_target_pairs={{0,15},{1,0},{2,1},{3,2},{4,3},{5,4},{6,5},{7,6},{8,7},{9,8},{10,9... | collective-permute-start | bytes 393224 | tf_op jit(solution)/shard_map/ppermute | solution.py:21
  151.5 3.5 collective-permute-start.17
  156.9 5.1 %collective-permute-start.33 = (bf16[64,1024]{1,0:T(8,128)(2,1)S(1)}, bf16[64,1024]{1,0:T(8,128)(2,1)S(1)}, u32[]{:S(2)}, u32[]{:S(2)}) collective-permute-start(bf16[64,1024]{1,0:T(8,128)(2,1)S(1)} %collective-permute-done.31), channel_id=1, source_target_pairs={{0,15},{1,0},{2,1},{3,2},{4,3},{5,4},{6,5},{7,6},{8,7},{9,8},{10,9... | collective-permute-start | bytes 393224 | tf_op jit(solution)/shard_map/ppermute | solution.py:21
  162.2 5.5 %collective-permute-start.18 = (f32[2,32,256]{2,1,0:T(8,128)S(1)}, f32[2,32,256]{2,1,0:T(8,128)S(1)}, u32[]{:S(2)}, u32[]{:S(2)}) collective-permute-start(f32[2,32,256]{2,1,0:T(8,128)S(1)} %dynamic-slice_bitcast_fusion.11), channel_id=1, source_target_pairs={{0,64},{16,80},{32,96},{48,112},{64,0},{80,16},{96,32},{112,48},{1... | collective-permute-start | bytes 196616 | tf_op jit(solution)/shard_map/ppermute | solution.py:49
  169.9 4.8 %collective-permute-start.19 = (f32[32,256]{1,0:T(8,128)S(1)}, f32[32,256]{1,0:T(8,128)S(1)}, u32[]{:S(2)}, u32[]{:S(2)}) collective-permute-start(f32[32,256]{1,0:T(8,128)S(1)} %dynamic-slice_bitcast_fusion.15), channel_id=1, source_target_pairs={{0,256},{16,272},{32,288},{48,304},{64,320},{80,336},{96,352},{112... | collective-permute-start | bytes 98312 | tf_op jit(solution)/shard_map/ppermute | solution.py:49
  174.7 2.5 collective-permute-done.19
  177.9 1.9 collective-permute-start.40
  179.9 5.1 %collective-permute-start.41 = (bf16[64,1024]{1,0:T(8,128)(2,1)S(1)}, bf16[64,1024]{1,0:T(8,128)(2,1)S(1)}, u32[]{:S(2)}, u32[]{:S(2)}) collective-permute-start(bf16[64,1024]{1,0:T(8,128)(2,1)S(1)} %bitcast.135), channel_id=1, source_target_pairs={{0,15},{1,0},{2,1},{3,2},{4,3},{5,4},{6,5},{7,6},{8,7},{9,8},{10,9... | collective-permute-start | bytes 393224 | tf_op jit(solution)/shard_map/ppermute | solution.py:21
  185.5 1.9 collective-permute-start.35
  187.8 1.9 collective-permute-start.42
  189.8 5.1 %collective-permute-start.43 = (bf16[64,1024]{1,0:T(8,128)(2,1)S(1)}, bf16[64,1024]{1,0:T(8,128)(2,1)S(1)}, u32[]{:S(2)}, u32[]{:S(2)}) collective-permute-start(bf16[64,1024]{1,0:T(8,128)(2,1)S(1)} %collective-permute-done.41), channel_id=1, source_target_pairs={{0,15},{1,0},{2,1},{3,2},{4,3},{5,4},{6,5},{7,6},{8,7},{9,8},{10,9... | collective-permute-start | bytes 393224 | tf_op jit(solution)/shard_map/ppermute | solution.py:21
  198.8 5.1 %collective-permute-start.45 = (bf16[64,1024]{1,0:T(8,128)(2,1)S(1)}, bf16[64,1024]{1,0:T(8,128)(2,1)S(1)}, u32[]{:S(2)}, u32[]{:S(2)}) collective-permute-start(bf16[64,1024]{1,0:T(8,128)(2,1)S(1)} %collective-permute-done.43), channel_id=1, source_target_pairs={{0,15},{1,0},{2,1},{3,2},{4,3},{5,4},{6,5},{7,6},{8,7},{9,8},{10,9... | collective-permute-start | bytes 393224 | tf_op jit(solution)/shard_map/ppermute | solution.py:21
  206.9 5.1 %collective-permute-start.47 = (bf16[64,1024]{1,0:T(8,128)(2,1)S(1)}, bf16[64,1024]{1,0:T(8,128)(2,1)S(1)}, u32[]{:S(2)}, u32[]{:S(2)}) collective-permute-start(bf16[64,1024]{1,0:T(8,128)(2,1)S(1)} %collective-permute-done.45), channel_id=1, source_target_pairs={{0,15},{1,0},{2,1},{3,2},{4,3},{5,4},{6,5},{7,6},{8,7},{9,8},{10,9... | collective-permute-start | bytes 393224 | tf_op jit(solution)/shard_map/ppermute | solution.py:21
  212.2 3.9 %collective-permute-start.36 = (f32[2,2,2,32,256]{4,3,2,1,0:T(8,128)S(1)}, f32[2,2,2,32,256]{4,3,2,1,0:T(8,128)S(1)}, u32[]{:S(2)}, u32[]{:S(2)}) collective-permute-start(f32[2,2,2,32,256]{4,3,2,1,0:T(8,128)S(1)} %dynamic-slice_bitcast_fusion.2), channel_id=1, source_target_pairs={{0,32},{16,48},{32,0},{48,16},{64,96},{80,112},{96,64},{112,80},{1... | collective-permute-start | bytes 786440 | tf_op jit(solution)/shard_map/ppermute | solution.py:49
  218.1 5.1 %collective-permute-start.49 = (bf16[64,1024]{1,0:T(8,128)(2,1)S(1)}, bf16[64,1024]{1,0:T(8,128)(2,1)S(1)}, u32[]{:S(2)}, u32[]{:S(2)}) collective-permute-start(bf16[64,1024]{1,0:T(8,128)(2,1)S(1)} %collective-permute-done.47), channel_id=1, source_target_pairs={{0,15},{1,0},{2,1},{3,2},{4,3},{5,4},{6,5},{7,6},{8,7},{9,8},{10,9... | collective-permute-start | bytes 393224 | tf_op jit(solution)/shard_map/ppermute | solution.py:21
  226.1 5.1 %collective-permute-start.51 = (bf16[64,1024]{1,0:T(8,128)(2,1)S(1)}, bf16[64,1024]{1,0:T(8,128)(2,1)S(1)}, u32[]{:S(2)}, u32[]{:S(2)}) collective-permute-start(bf16[64,1024]{1,0:T(8,128)(2,1)S(1)} %collective-permute-done.49), channel_id=1, source_target_pairs={{0,15},{1,0},{2,1},{3,2},{4,3},{5,4},{6,5},{7,6},{8,7},{9,8},{10,9... | collective-permute-start | bytes 393224 | tf_op jit(solution)/shard_map/ppermute | solution.py:21
  231.4 2.4 collective-permute-start.37
  235.7 5.1 %collective-permute-start.53 = (bf16[64,1024]{1,0:T(8,128)(2,1)S(1)}, bf16[64,1024]{1,0:T(8,128)(2,1)S(1)}, u32[]{:S(2)}, u32[]{:S(2)}) collective-permute-start(bf16[64,1024]{1,0:T(8,128)(2,1)S(1)} %collective-permute-done.51), channel_id=1, source_target_pairs={{0,15},{1,0},{2,1},{3,2},{4,3},{5,4},{6,5},{7,6},{8,7},{9,8},{10,9... | collective-permute-start | bytes 393224 | tf_op jit(solution)/shard_map/ppermute | solution.py:21
  240.9 4.0 %collective-permute-start.38 = (f32[2,32,256]{2,1,0:T(8,128)S(1)}, f32[2,32,256]{2,1,0:T(8,128)S(1)}, u32[]{:S(2)}, u32[]{:S(2)}) collective-permute-start(f32[2,32,256]{2,1,0:T(8,128)S(1)} %dynamic-slice_bitcast_fusion.10), channel_id=1, source_target_pairs={{0,64},{16,80},{32,96},{48,112},{64,0},{80,16},{96,32},{112,48},{1... | collective-permute-start | bytes 196616 | tf_op jit(solution)/shard_map/ppermute | solution.py:49
  245.0 1.9 collective-permute-start.54
  248.6 5.1 %collective-permute-start.39 = (f32[32,256]{1,0:T(8,128)S(1)}, f32[32,256]{1,0:T(8,128)S(1)}, u32[]{:S(2)}, u32[]{:S(2)}) collective-permute-start(f32[32,256]{1,0:T(8,128)S(1)} %dynamic-slice_bitcast_fusion.14), channel_id=1, source_target_pairs={{0,256},{16,272},{32,288},{48,304},{64,320},{80,336},{96,352},{112... | collective-permute-start | bytes 98312 | tf_op jit(solution)/shard_map/ppermute | solution.py:49
  253.8 2.2 collective-permute-done.39
  258.6 5.1 %collective-permute-start.61 = (bf16[64,1024]{1,0:T(8,128)(2,1)S(1)}, bf16[64,1024]{1,0:T(8,128)(2,1)S(1)}, u32[]{:S(2)}, u32[]{:S(2)}) collective-permute-start(bf16[64,1024]{1,0:T(8,128)(2,1)S(1)} %bitcast.132), channel_id=1, source_target_pairs={{0,15},{1,0},{2,1},{3,2},{4,3},{5,4},{6,5},{7,6},{8,7},{9,8},{10,9... | collective-permute-start | bytes 393224 | tf_op jit(solution)/shard_map/ppermute | solution.py:21
  268.5 5.1 %collective-permute-start.63 = (bf16[64,1024]{1,0:T(8,128)(2,1)S(1)}, bf16[64,1024]{1,0:T(8,128)(2,1)S(1)}, u32[]{:S(2)}, u32[]{:S(2)}) collective-permute-start(bf16[64,1024]{1,0:T(8,128)(2,1)S(1)} %collective-permute-done.61), channel_id=1, source_target_pairs={{0,15},{1,0},{2,1},{3,2},{4,3},{5,4},{6,5},{7,6},{8,7},{9,8},{10,9... | collective-permute-start | bytes 393224 | tf_op jit(solution)/shard_map/ppermute | solution.py:21
  277.5 5.1 %collective-permute-start.65 = (bf16[64,1024]{1,0:T(8,128)(2,1)S(1)}, bf16[64,1024]{1,0:T(8,128)(2,1)S(1)}, u32[]{:S(2)}, u32[]{:S(2)}) collective-permute-start(bf16[64,1024]{1,0:T(8,128)(2,1)S(1)} %collective-permute-done.63), channel_id=1, source_target_pairs={{0,15},{1,0},{2,1},{3,2},{4,3},{5,4},{6,5},{7,6},{8,7},{9,8},{10,9... | collective-permute-start | bytes 393224 | tf_op jit(solution)/shard_map/ppermute | solution.py:21
  285.6 5.1 %collective-permute-start.67 = (bf16[64,1024]{1,0:T(8,128)(2,1)S(1)}, bf16[64,1024]{1,0:T(8,128)(2,1)S(1)}, u32[]{:S(2)}, u32[]{:S(2)}) collective-permute-start(bf16[64,1024]{1,0:T(8,128)(2,1)S(1)} %collective-permute-done.65), channel_id=1, source_target_pairs={{0,15},{1,0},{2,1},{3,2},{4,3},{5,4},{6,5},{7,6},{8,7},{9,8},{10,9... | collective-permute-start | bytes 393224 | tf_op jit(solution)/shard_map/ppermute | solution.py:21
  290.9 1.9 collective-permute-start.56
  294.9 5.1 %collective-permute-start.69 = (bf16[64,1024]{1,0:T(8,128)(2,1)S(1)}, bf16[64,1024]{1,0:T(8,128)(2,1)S(1)}, u32[]{:S(2)}, u32[]{:S(2)}) collective-permute-start(bf16[64,1024]{1,0:T(8,128)(2,1)S(1)} %collective-permute-done.67), channel_id=1, source_target_pairs={{0,15},{1,0},{2,1},{3,2},{4,3},{5,4},{6,5},{7,6},{8,7},{9,8},{10,9... | collective-permute-start | bytes 393224 | tf_op jit(solution)/shard_map/ppermute | solution.py:21
  302.9 5.1 %collective-permute-start.71 = (bf16[64,1024]{1,0:T(8,128)(2,1)S(1)}, bf16[64,1024]{1,0:T(8,128)(2,1)S(1)}, u32[]{:S(2)}, u32[]{:S(2)}) collective-permute-start(bf16[64,1024]{1,0:T(8,128)(2,1)S(1)} %collective-permute-done.69), channel_id=1, source_target_pairs={{0,15},{1,0},{2,1},{3,2},{4,3},{5,4},{6,5},{7,6},{8,7},{9,8},{10,9... | collective-permute-start | bytes 393224 | tf_op jit(solution)/shard_map/ppermute | solution.py:21
  311.0 5.1 %collective-permute-start.73 = (bf16[64,1024]{1,0:T(8,128)(2,1)S(1)}, bf16[64,1024]{1,0:T(8,128)(2,1)S(1)}, u32[]{:S(2)}, u32[]{:S(2)}) collective-permute-start(bf16[64,1024]{1,0:T(8,128)(2,1)S(1)} %collective-permute-done.71), channel_id=1, source_target_pairs={{0,15},{1,0},{2,1},{3,2},{4,3},{5,4},{6,5},{7,6},{8,7},{9,8},{10,9... | collective-permute-start | bytes 393224 | tf_op jit(solution)/shard_map/ppermute | solution.py:21
  319.1 6.1 %collective-permute-done.74 = bf16[64,1024]{1,0:T(8,128)(2,1)S(1)} collective-permute-done((bf16[64,1024]{1,0:T(8,128)(2,1)S(1)}, bf16[64,1024]{1,0:T(8,128)(2,1)S(1)}, u32[]{:S(2)}, u32[]{:S(2)}) %collective-permute-start.74) | collective-permute-done | bytes 131104 | tf_op jit(solution)/shard_map/ppermute | solution.py:18
  329.4 3.5 collective-permute-start.57
  333.1 3.9 %collective-permute-start.76 = (f32[2,2,2,40,256]{4,3,2,1,0:T(8,128)S(1)}, f32[2,2,2,40,256]{4,3,2,1,0:T(8,128)S(1)}, u32[]{:S(2)}, u32[]{:S(2)}) collective-permute-start(f32[2,2,2,40,256]{4,3,2,1,0:T(8,128)S(1)} %dynamic-slice_bitcast_fusion), channel_id=1, source_target_pairs={{0,32},{16,48},{32,0},{48,16},{64,96},{80,112},{96,64},{112,80},{1... | collective-permute-start | bytes 983048 | tf_op jit(solution)/shard_map/ppermute | solution.py:49
  337.3 5.4 %collective-permute-start.58 = (f32[2,32,256]{2,1,0:T(8,128)S(1)}, f32[2,32,256]{2,1,0:T(8,128)S(1)}, u32[]{:S(2)}, u32[]{:S(2)}) collective-permute-start(f32[2,32,256]{2,1,0:T(8,128)S(1)} %dynamic-slice_bitcast_fusion.9), channel_id=1, source_target_pairs={{0,64},{16,80},{32,96},{48,112},{64,0},{80,16},{96,32},{112,48},{1... | collective-permute-start | bytes 196616 | tf_op jit(solution)/shard_map/ppermute | solution.py:49
  342.7 2.8 collective-permute-done.76
  345.6 2.4 collective-permute-start.77
  348.3 4.5 %collective-permute-done.77 = f32[2,2,40,256]{3,2,1,0:T(8,128)S(1)} collective-permute-done((f32[2,2,40,256]{3,2,1,0:T(8,128)S(1)}, f32[2,2,40,256]{3,2,1,0:T(8,128)S(1)}, u32[]{:S(2)}, u32[]{:S(2)}) %collective-permute-start.77) | collective-permute-done | bytes 163872 | tf_op jit(solution)/shard_map/ppermute | solution.py:49
  352.9 5.4 %collective-permute-start.78 = (f32[2,40,256]{2,1,0:T(8,128)S(1)}, f32[2,40,256]{2,1,0:T(8,128)S(1)}, u32[]{:S(2)}, u32[]{:S(2)}) collective-permute-start(f32[2,40,256]{2,1,0:T(8,128)S(1)} %dynamic-slice_bitcast_fusion.8), channel_id=1, source_target_pairs={{0,64},{16,80},{32,96},{48,112},{64,0},{80,16},{96,32},{112,48},{1... | collective-permute-start | bytes 245768 | tf_op jit(solution)/shard_map/ppermute | solution.py:49
  358.3 4.8 %collective-permute-start.59 = (f32[32,256]{1,0:T(8,128)S(1)}, f32[32,256]{1,0:T(8,128)S(1)}, u32[]{:S(2)}, u32[]{:S(2)}) collective-permute-start(f32[32,256]{1,0:T(8,128)S(1)} %dynamic-slice_bitcast_fusion.13), channel_id=1, source_target_pairs={{0,256},{16,272},{32,288},{48,304},{64,320},{80,336},{96,352},{112... | collective-permute-start | bytes 98312 | tf_op jit(solution)/shard_map/ppermute | solution.py:49
  363.2 2.5 collective-permute-start.79
  365.7 4.8 %collective-permute-done.79 = f32[40,256]{1,0:T(8,128)S(1)} collective-permute-done((f32[40,256]{1,0:T(8,128)S(1)}, f32[40,256]{1,0:T(8,128)S(1)}, u32[]{:S(2)}, u32[]{:S(2)}) %collective-permute-start.79) | collective-permute-done | bytes 40992 | tf_op jit(solution)/shard_map/ppermute | solution.py:49
  (253 shorter events, 96.4 us)
Async XLA Ops:
  11.4 16.7 %collective-permute-start.82 = (f32[8,384]{1,0:T(8,128)S(1)}, f32[8,384]{1,0:T(8,128)S(1)}, u32[]{:S(2)}, u32[]{:S(2)}) collective-permute-start(f32[8,384]{1,0:T(8,128)S(1)} %add.460), channel_id=1, source_target_pairs={{0,64},{16,80},{32,96},{48,112},{64,0},{80,16},{96,32},{112,48},{1... | collective-permute-start | bytes 36872 | tf_op jit(solution)/shard_map/ppermute | solution.py:32
  18.6 22.2 %collective-permute-start = (bf16[64,1024]{1,0:T(8,128)(2,1)S(1)}, bf16[64,1024]{1,0:T(8,128)(2,1)S(1)}, u32[]{:S(2)}, u32[]{:S(2)}) collective-permute-start(bf16[64,1024]{1,0:T(8,128)(2,1)S(1)} %bitcast.140), channel_id=1, source_target_pairs={{0,1},{1,2},{2,3},{3,4},{4,5},{5,6},{6,7},{7,8},{8,9},{9,10},{10,1... | collective-permute-start | bytes 393224 | tf_op jit(solution)/shard_map/ppermute | solution.py:18
  20.6 22.2 %collective-permute-start.1 = (bf16[64,1024]{1,0:T(8,128)(2,1)S(1)}, bf16[64,1024]{1,0:T(8,128)(2,1)S(1)}, u32[]{:S(2)}, u32[]{:S(2)}) collective-permute-start(bf16[64,1024]{1,0:T(8,128)(2,1)S(1)} %bitcast.141), channel_id=1, source_target_pairs={{0,15},{1,0},{2,1},{3,2},{4,3},{5,4},{6,5},{7,6},{8,7},{9,8},{10,9... | collective-permute-start | bytes 393224 | tf_op jit(solution)/shard_map/ppermute | solution.py:21
  40.8 8.1 %collective-permute-start.2 = (bf16[64,1024]{1,0:T(8,128)(2,1)S(1)}, bf16[64,1024]{1,0:T(8,128)(2,1)S(1)}, u32[]{:S(2)}, u32[]{:S(2)}) collective-permute-start(bf16[64,1024]{1,0:T(8,128)(2,1)S(1)} %collective-permute-done), channel_id=1, source_target_pairs={{0,1},{1,2},{2,3},{3,4},{4,5},{5,6},{6,7},{7,8},{8,9},{9,10},{10,1... | collective-permute-start | bytes 393224 | tf_op jit(solution)/shard_map/ppermute | solution.py:18
  48.9 8.5 %collective-permute-start.4 = (bf16[64,1024]{1,0:T(8,128)(2,1)S(1)}, bf16[64,1024]{1,0:T(8,128)(2,1)S(1)}, u32[]{:S(2)}, u32[]{:S(2)}) collective-permute-start(bf16[64,1024]{1,0:T(8,128)(2,1)S(1)} %collective-permute-done.2), channel_id=1, source_target_pairs={{0,1},{1,2},{2,3},{3,4},{4,5},{5,6},{6,7},{7,8},{8,9},{9,10},{10,1... | collective-permute-start | bytes 393224 | tf_op jit(solution)/shard_map/ppermute | solution.py:18
  50.8 8.5 %collective-permute-start.5 = (bf16[64,1024]{1,0:T(8,128)(2,1)S(1)}, bf16[64,1024]{1,0:T(8,128)(2,1)S(1)}, u32[]{:S(2)}, u32[]{:S(2)}) collective-permute-start(bf16[64,1024]{1,0:T(8,128)(2,1)S(1)} %collective-permute-done.3), channel_id=1, source_target_pairs={{0,15},{1,0},{2,1},{3,2},{4,3},{5,4},{6,5},{7,6},{8,7},{9,8},{10,9... | collective-permute-start | bytes 393224 | tf_op jit(solution)/shard_map/ppermute | solution.py:21
  57.4 9.3 %collective-permute-start.6 = (bf16[64,1024]{1,0:T(8,128)(2,1)S(1)}, bf16[64,1024]{1,0:T(8,128)(2,1)S(1)}, u32[]{:S(2)}, u32[]{:S(2)}) collective-permute-start(bf16[64,1024]{1,0:T(8,128)(2,1)S(1)} %collective-permute-done.4), channel_id=1, source_target_pairs={{0,1},{1,2},{2,3},{3,4},{4,5},{5,6},{6,7},{7,8},{8,9},{9,10},{10,1... | collective-permute-start | bytes 393224 | tf_op jit(solution)/shard_map/ppermute | solution.py:18
  59.4 9.3 %collective-permute-start.7 = (bf16[64,1024]{1,0:T(8,128)(2,1)S(1)}, bf16[64,1024]{1,0:T(8,128)(2,1)S(1)}, u32[]{:S(2)}, u32[]{:S(2)}) collective-permute-start(bf16[64,1024]{1,0:T(8,128)(2,1)S(1)} %collective-permute-done.5), channel_id=1, source_target_pairs={{0,15},{1,0},{2,1},{3,2},{4,3},{5,4},{6,5},{7,6},{8,7},{9,8},{10,9... | collective-permute-start | bytes 393224 | tf_op jit(solution)/shard_map/ppermute | solution.py:21
  66.7 8.4 %collective-permute-start.8 = (bf16[64,1024]{1,0:T(8,128)(2,1)S(1)}, bf16[64,1024]{1,0:T(8,128)(2,1)S(1)}, u32[]{:S(2)}, u32[]{:S(2)}) collective-permute-start(bf16[64,1024]{1,0:T(8,128)(2,1)S(1)} %collective-permute-done.6), channel_id=1, source_target_pairs={{0,1},{1,2},{2,3},{3,4},{4,5},{5,6},{6,7},{7,8},{8,9},{9,10},{10,1... | collective-permute-start | bytes 393224 | tf_op jit(solution)/shard_map/ppermute | solution.py:18
  68.6 8.4 %collective-permute-start.9 = (bf16[64,1024]{1,0:T(8,128)(2,1)S(1)}, bf16[64,1024]{1,0:T(8,128)(2,1)S(1)}, u32[]{:S(2)}, u32[]{:S(2)}) collective-permute-start(bf16[64,1024]{1,0:T(8,128)(2,1)S(1)} %collective-permute-done.7), channel_id=1, source_target_pairs={{0,15},{1,0},{2,1},{3,2},{4,3},{5,4},{6,5},{7,6},{8,7},{9,8},{10,9... | collective-permute-start | bytes 393224 | tf_op jit(solution)/shard_map/ppermute | solution.py:21
  75.1 8.1 %collective-permute-start.10 = (bf16[64,1024]{1,0:T(8,128)(2,1)S(1)}, bf16[64,1024]{1,0:T(8,128)(2,1)S(1)}, u32[]{:S(2)}, u32[]{:S(2)}) collective-permute-start(bf16[64,1024]{1,0:T(8,128)(2,1)S(1)} %collective-permute-done.8), channel_id=1, source_target_pairs={{0,1},{1,2},{2,3},{3,4},{4,5},{5,6},{6,7},{7,8},{8,9},{9,10},{10,1... | collective-permute-start | bytes 393224 | tf_op jit(solution)/shard_map/ppermute | solution.py:18
  83.2 8.1 %collective-permute-start.12 = (bf16[64,1024]{1,0:T(8,128)(2,1)S(1)}, bf16[64,1024]{1,0:T(8,128)(2,1)S(1)}, u32[]{:S(2)}, u32[]{:S(2)}) collective-permute-start(bf16[64,1024]{1,0:T(8,128)(2,1)S(1)} %collective-permute-done.10), channel_id=1, source_target_pairs={{0,1},{1,2},{2,3},{3,4},{4,5},{5,6},{6,7},{7,8},{8,9},{9,10},{10,1... | collective-permute-start | bytes 393224 | tf_op jit(solution)/shard_map/ppermute | solution.py:18
  85.1 8.1 %collective-permute-start.13 = (bf16[64,1024]{1,0:T(8,128)(2,1)S(1)}, bf16[64,1024]{1,0:T(8,128)(2,1)S(1)}, u32[]{:S(2)}, u32[]{:S(2)}) collective-permute-start(bf16[64,1024]{1,0:T(8,128)(2,1)S(1)} %collective-permute-done.11), channel_id=1, source_target_pairs={{0,15},{1,0},{2,1},{3,2},{4,3},{5,4},{6,5},{7,6},{8,7},{9,8},{10,9... | collective-permute-start | bytes 393224 | tf_op jit(solution)/shard_map/ppermute | solution.py:21
  91.2 8.1 %collective-permute-start.14 = (bf16[64,1024]{1,0:T(8,128)(2,1)S(1)}, bf16[64,1024]{1,0:T(8,128)(2,1)S(1)}, u32[]{:S(2)}, u32[]{:S(2)}) collective-permute-start(bf16[64,1024]{1,0:T(8,128)(2,1)S(1)} %collective-permute-done.12), channel_id=1, source_target_pairs={{0,1},{1,2},{2,3},{3,4},{4,5},{5,6},{6,7},{7,8},{8,9},{9,10},{10,1... | collective-permute-start | bytes 393224 | tf_op jit(solution)/shard_map/ppermute | solution.py:18
  100.0 9.8 %collective-permute-start.20 = (bf16[64,1024]{1,0:T(8,128)(2,1)S(1)}, bf16[64,1024]{1,0:T(8,128)(2,1)S(1)}, u32[]{:S(2)}, u32[]{:S(2)}) collective-permute-start(bf16[64,1024]{1,0:T(8,128)(2,1)S(1)} %bitcast.137), channel_id=1, source_target_pairs={{0,1},{1,2},{2,3},{3,4},{4,5},{5,6},{6,7},{7,8},{8,9},{9,10},{10,1... | collective-permute-start | bytes 393224 | tf_op jit(solution)/shard_map/ppermute | solution.py:18
  102.0 9.8 %collective-permute-start.21 = (bf16[64,1024]{1,0:T(8,128)(2,1)S(1)}, bf16[64,1024]{1,0:T(8,128)(2,1)S(1)}, u32[]{:S(2)}, u32[]{:S(2)}) collective-permute-start(bf16[64,1024]{1,0:T(8,128)(2,1)S(1)} %bitcast.138), channel_id=1, source_target_pairs={{0,15},{1,0},{2,1},{3,2},{4,3},{5,4},{6,5},{7,6},{8,7},{9,8},{10,9... | collective-permute-start | bytes 393224 | tf_op jit(solution)/shard_map/ppermute | solution.py:21
  107.6 34.6 %collective-permute-start.15 = (f32[2,2,2,2,32,256]{5,4,2,1,0,3:T(8,128)S(1)}, f32[2,2,2,2,32,256]{5,4,2,1,0,3:T(8,128)S(1)}, u32[]{:S(2)}, u32[]{:S(2)}) collective-permute-start(f32[2,2,2,2,32,256]{5,4,2,1,0,3:T(8,128)S(1)} %bitcast.128), channel_id=1, source_target_pairs={{0,16},{16,0},{32,48},{48,32},{64,80},{80,64},{96,112},{112,96},{1... | collective-permute-start | bytes 1572872 | tf_op jit(solution)/shard_map/ppermute | solution.py:49
  109.9 9.0 %collective-permute-start.22 = (bf16[64,1024]{1,0:T(8,128)(2,1)S(1)}, bf16[64,1024]{1,0:T(8,128)(2,1)S(1)}, u32[]{:S(2)}, u32[]{:S(2)}) collective-permute-start(bf16[64,1024]{1,0:T(8,128)(2,1)S(1)} %collective-permute-done.20), channel_id=1, source_target_pairs={{0,1},{1,2},{2,3},{3,4},{4,5},{5,6},{6,7},{7,8},{8,9},{9,10},{10,1... | collective-permute-start | bytes 393224 | tf_op jit(solution)/shard_map/ppermute | solution.py:18
  111.8 9.0 %collective-permute-start.23 = (bf16[64,1024]{1,0:T(8,128)(2,1)S(1)}, bf16[64,1024]{1,0:T(8,128)(2,1)S(1)}, u32[]{:S(2)}, u32[]{:S(2)}) collective-permute-start(bf16[64,1024]{1,0:T(8,128)(2,1)S(1)} %collective-permute-done.21), channel_id=1, source_target_pairs={{0,15},{1,0},{2,1},{3,2},{4,3},{5,4},{6,5},{7,6},{8,7},{9,8},{10,9... | collective-permute-start | bytes 393224 | tf_op jit(solution)/shard_map/ppermute | solution.py:21
  118.9 8.1 %collective-permute-start.24 = (bf16[64,1024]{1,0:T(8,128)(2,1)S(1)}, bf16[64,1024]{1,0:T(8,128)(2,1)S(1)}, u32[]{:S(2)}, u32[]{:S(2)}) collective-permute-start(bf16[64,1024]{1,0:T(8,128)(2,1)S(1)} %collective-permute-done.22), channel_id=1, source_target_pairs={{0,1},{1,2},{2,3},{3,4},{4,5},{5,6},{6,7},{7,8},{8,9},{9,10},{10,1... | collective-permute-start | bytes 393224 | tf_op jit(solution)/shard_map/ppermute | solution.py:18
  120.8 8.1 %collective-permute-start.25 = (bf16[64,1024]{1,0:T(8,128)(2,1)S(1)}, bf16[64,1024]{1,0:T(8,128)(2,1)S(1)}, u32[]{:S(2)}, u32[]{:S(2)}) collective-permute-start(bf16[64,1024]{1,0:T(8,128)(2,1)S(1)} %collective-permute-done.23), channel_id=1, source_target_pairs={{0,15},{1,0},{2,1},{3,2},{4,3},{5,4},{6,5},{7,6},{8,7},{9,8},{10,9... | collective-permute-start | bytes 393224 | tf_op jit(solution)/shard_map/ppermute | solution.py:21
  127.0 8.1 %collective-permute-start.26 = (bf16[64,1024]{1,0:T(8,128)(2,1)S(1)}, bf16[64,1024]{1,0:T(8,128)(2,1)S(1)}, u32[]{:S(2)}, u32[]{:S(2)}) collective-permute-start(bf16[64,1024]{1,0:T(8,128)(2,1)S(1)} %collective-permute-done.24), channel_id=1, source_target_pairs={{0,1},{1,2},{2,3},{3,4},{4,5},{5,6},{6,7},{7,8},{8,9},{9,10},{10,1... | collective-permute-start | bytes 393224 | tf_op jit(solution)/shard_map/ppermute | solution.py:18
  135.1 9.2 %collective-permute-start.28 = (bf16[64,1024]{1,0:T(8,128)(2,1)S(1)}, bf16[64,1024]{1,0:T(8,128)(2,1)S(1)}, u32[]{:S(2)}, u32[]{:S(2)}) collective-permute-start(bf16[64,1024]{1,0:T(8,128)(2,1)S(1)} %collective-permute-done.26), channel_id=1, source_target_pairs={{0,1},{1,2},{2,3},{3,4},{4,5},{5,6},{6,7},{7,8},{8,9},{9,10},{10,1... | collective-permute-start | bytes 393224 | tf_op jit(solution)/shard_map/ppermute | solution.py:18
  137.0 9.2 %collective-permute-start.29 = (bf16[64,1024]{1,0:T(8,128)(2,1)S(1)}, bf16[64,1024]{1,0:T(8,128)(2,1)S(1)}, u32[]{:S(2)}, u32[]{:S(2)}) collective-permute-start(bf16[64,1024]{1,0:T(8,128)(2,1)S(1)} %collective-permute-done.27), channel_id=1, source_target_pairs={{0,15},{1,0},{2,1},{3,2},{4,3},{5,4},{6,5},{7,6},{8,7},{9,8},{10,9... | collective-permute-start | bytes 393224 | tf_op jit(solution)/shard_map/ppermute | solution.py:21
  142.3 9.1 %collective-permute-start.16 = (f32[2,2,2,32,256]{4,3,2,1,0:T(8,128)S(1)}, f32[2,2,2,32,256]{4,3,2,1,0:T(8,128)S(1)}, u32[]{:S(2)}, u32[]{:S(2)}) collective-permute-start(f32[2,2,2,32,256]{4,3,2,1,0:T(8,128)S(1)} %dynamic-slice_bitcast_fusion.3), channel_id=1, source_target_pairs={{0,32},{16,48},{32,0},{48,16},{64,96},{80,112},{96,64},{112,80},{1... | collective-permute-start | bytes 786440 | tf_op jit(solution)/shard_map/ppermute | solution.py:49
  144.2 10.7 %collective-permute-start.30 = (bf16[64,1024]{1,0:T(8,128)(2,1)S(1)}, bf16[64,1024]{1,0:T(8,128)(2,1)S(1)}, u32[]{:S(2)}, u32[]{:S(2)}) collective-permute-start(bf16[64,1024]{1,0:T(8,128)(2,1)S(1)} %collective-permute-done.28), channel_id=1, source_target_pairs={{0,1},{1,2},{2,3},{3,4},{4,5},{5,6},{6,7},{7,8},{8,9},{9,10},{10,1... | collective-permute-start | bytes 393224 | tf_op jit(solution)/shard_map/ppermute | solution.py:18
  146.2 10.7 %collective-permute-start.31 = (bf16[64,1024]{1,0:T(8,128)(2,1)S(1)}, bf16[64,1024]{1,0:T(8,128)(2,1)S(1)}, u32[]{:S(2)}, u32[]{:S(2)}) collective-permute-start(bf16[64,1024]{1,0:T(8,128)(2,1)S(1)} %collective-permute-done.29), channel_id=1, source_target_pairs={{0,15},{1,0},{2,1},{3,2},{4,3},{5,4},{6,5},{7,6},{8,7},{9,8},{10,9... | collective-permute-start | bytes 393224 | tf_op jit(solution)/shard_map/ppermute | solution.py:21
  151.5 10.6 %collective-permute-start.17 = (f32[2,2,32,256]{3,2,1,0:T(8,128)S(1)}, f32[2,2,32,256]{3,2,1,0:T(8,128)S(1)}, u32[]{:S(2)}, u32[]{:S(2)}) collective-permute-start(f32[2,2,32,256]{3,2,1,0:T(8,128)S(1)} %dynamic-slice_bitcast_fusion.7), channel_id=1, source_target_pairs={{0,128},{16,144},{32,160},{48,176},{64,192},{80,208},{96,224},{112... | collective-permute-start | bytes 393224 | tf_op jit(solution)/shard_map/ppermute | solution.py:49
  155.0 12.7 %collective-permute-start.32 = (bf16[64,1024]{1,0:T(8,128)(2,1)S(1)}, bf16[64,1024]{1,0:T(8,128)(2,1)S(1)}, u32[]{:S(2)}, u32[]{:S(2)}) collective-permute-start(bf16[64,1024]{1,0:T(8,128)(2,1)S(1)} %collective-permute-done.30), channel_id=1, source_target_pairs={{0,1},{1,2},{2,3},{3,4},{4,5},{5,6},{6,7},{7,8},{8,9},{9,10},{10,1... | collective-permute-start | bytes 393224 | tf_op jit(solution)/shard_map/ppermute | solution.py:18
  156.9 17.8 %collective-permute-start.33 = (bf16[64,1024]{1,0:T(8,128)(2,1)S(1)}, bf16[64,1024]{1,0:T(8,128)(2,1)S(1)}, u32[]{:S(2)}, u32[]{:S(2)}) collective-permute-start(bf16[64,1024]{1,0:T(8,128)(2,1)S(1)} %collective-permute-done.31), channel_id=1, source_target_pairs={{0,15},{1,0},{2,1},{3,2},{4,3},{5,4},{6,5},{7,6},{8,7},{9,8},{10,9... | collective-permute-start | bytes 393224 | tf_op jit(solution)/shard_map/ppermute | solution.py:21
  167.6 9.6 %collective-permute-start.34 = (bf16[64,1024]{1,0:T(8,128)(2,1)S(1)}, bf16[64,1024]{1,0:T(8,128)(2,1)S(1)}, u32[]{:S(2)}, u32[]{:S(2)}) collective-permute-start(bf16[64,1024]{1,0:T(8,128)(2,1)S(1)} %collective-permute-done.32), channel_id=1, source_target_pairs={{0,1},{1,2},{2,3},{3,4},{4,5},{5,6},{6,7},{7,8},{8,9},{9,10},{10,1... | collective-permute-start | bytes 393224 | tf_op jit(solution)/shard_map/ppermute | solution.py:18
  177.9 9.9 %collective-permute-start.40 = (bf16[64,1024]{1,0:T(8,128)(2,1)S(1)}, bf16[64,1024]{1,0:T(8,128)(2,1)S(1)}, u32[]{:S(2)}, u32[]{:S(2)}) collective-permute-start(bf16[64,1024]{1,0:T(8,128)(2,1)S(1)} %bitcast.134), channel_id=1, source_target_pairs={{0,1},{1,2},{2,3},{3,4},{4,5},{5,6},{6,7},{7,8},{8,9},{9,10},{10,1... | collective-permute-start | bytes 393224 | tf_op jit(solution)/shard_map/ppermute | solution.py:18
  179.9 9.9 %collective-permute-start.41 = (bf16[64,1024]{1,0:T(8,128)(2,1)S(1)}, bf16[64,1024]{1,0:T(8,128)(2,1)S(1)}, u32[]{:S(2)}, u32[]{:S(2)}) collective-permute-start(bf16[64,1024]{1,0:T(8,128)(2,1)S(1)} %bitcast.135), channel_id=1, source_target_pairs={{0,15},{1,0},{2,1},{3,2},{4,3},{5,4},{6,5},{7,6},{8,7},{9,8},{10,9... | collective-permute-start | bytes 393224 | tf_op jit(solution)/shard_map/ppermute | solution.py:21
  185.5 26.6 %collective-permute-start.35 = (f32[2,2,2,2,32,256]{5,4,2,1,0,3:T(8,128)S(1)}, f32[2,2,2,2,32,256]{5,4,2,1,0,3:T(8,128)S(1)}, u32[]{:S(2)}, u32[]{:S(2)}) collective-permute-start(f32[2,2,2,2,32,256]{5,4,2,1,0,3:T(8,128)S(1)} %bitcast.130), channel_id=1, source_target_pairs={{0,16},{16,0},{32,48},{48,32},{64,80},{80,64},{96,112},{112,96},{1... | collective-permute-start | bytes 1572872 | tf_op jit(solution)/shard_map/ppermute | solution.py:49
  187.8 9.0 %collective-permute-start.42 = (bf16[64,1024]{1,0:T(8,128)(2,1)S(1)}, bf16[64,1024]{1,0:T(8,128)(2,1)S(1)}, u32[]{:S(2)}, u32[]{:S(2)}) collective-permute-start(bf16[64,1024]{1,0:T(8,128)(2,1)S(1)} %collective-permute-done.40), channel_id=1, source_target_pairs={{0,1},{1,2},{2,3},{3,4},{4,5},{5,6},{6,7},{7,8},{8,9},{9,10},{10,1... | collective-permute-start | bytes 393224 | tf_op jit(solution)/shard_map/ppermute | solution.py:18
  189.8 9.0 %collective-permute-start.43 = (bf16[64,1024]{1,0:T(8,128)(2,1)S(1)}, bf16[64,1024]{1,0:T(8,128)(2,1)S(1)}, u32[]{:S(2)}, u32[]{:S(2)}) collective-permute-start(bf16[64,1024]{1,0:T(8,128)(2,1)S(1)} %collective-permute-done.41), channel_id=1, source_target_pairs={{0,15},{1,0},{2,1},{3,2},{4,3},{5,4},{6,5},{7,6},{8,7},{9,8},{10,9... | collective-permute-start | bytes 393224 | tf_op jit(solution)/shard_map/ppermute | solution.py:21
  196.8 8.1 %collective-permute-start.44 = (bf16[64,1024]{1,0:T(8,128)(2,1)S(1)}, bf16[64,1024]{1,0:T(8,128)(2,1)S(1)}, u32[]{:S(2)}, u32[]{:S(2)}) collective-permute-start(bf16[64,1024]{1,0:T(8,128)(2,1)S(1)} %collective-permute-done.42), channel_id=1, source_target_pairs={{0,1},{1,2},{2,3},{3,4},{4,5},{5,6},{6,7},{7,8},{8,9},{9,10},{10,1... | collective-permute-start | bytes 393224 | tf_op jit(solution)/shard_map/ppermute | solution.py:18
  198.8 8.1 %collective-permute-start.45 = (bf16[64,1024]{1,0:T(8,128)(2,1)S(1)}, bf16[64,1024]{1,0:T(8,128)(2,1)S(1)}, u32[]{:S(2)}, u32[]{:S(2)}) collective-permute-start(bf16[64,1024]{1,0:T(8,128)(2,1)S(1)} %collective-permute-done.43), channel_id=1, source_target_pairs={{0,15},{1,0},{2,1},{3,2},{4,3},{5,4},{6,5},{7,6},{8,7},{9,8},{10,9... | collective-permute-start | bytes 393224 | tf_op jit(solution)/shard_map/ppermute | solution.py:21
  205.0 11.1 %collective-permute-start.46 = (bf16[64,1024]{1,0:T(8,128)(2,1)S(1)}, bf16[64,1024]{1,0:T(8,128)(2,1)S(1)}, u32[]{:S(2)}, u32[]{:S(2)}) collective-permute-start(bf16[64,1024]{1,0:T(8,128)(2,1)S(1)} %collective-permute-done.44), channel_id=1, source_target_pairs={{0,1},{1,2},{2,3},{3,4},{4,5},{5,6},{6,7},{7,8},{8,9},{9,10},{10,1... | collective-permute-start | bytes 393224 | tf_op jit(solution)/shard_map/ppermute | solution.py:18
  206.9 11.2 %collective-permute-start.47 = (bf16[64,1024]{1,0:T(8,128)(2,1)S(1)}, bf16[64,1024]{1,0:T(8,128)(2,1)S(1)}, u32[]{:S(2)}, u32[]{:S(2)}) collective-permute-start(bf16[64,1024]{1,0:T(8,128)(2,1)S(1)} %collective-permute-done.45), channel_id=1, source_target_pairs={{0,15},{1,0},{2,1},{3,2},{4,3},{5,4},{6,5},{7,6},{8,7},{9,8},{10,9... | collective-permute-start | bytes 393224 | tf_op jit(solution)/shard_map/ppermute | solution.py:21
  212.2 19.1 %collective-permute-start.36 = (f32[2,2,2,32,256]{4,3,2,1,0:T(8,128)S(1)}, f32[2,2,2,32,256]{4,3,2,1,0:T(8,128)S(1)}, u32[]{:S(2)}, u32[]{:S(2)}) collective-permute-start(f32[2,2,2,32,256]{4,3,2,1,0:T(8,128)S(1)} %dynamic-slice_bitcast_fusion.2), channel_id=1, source_target_pairs={{0,32},{16,48},{32,0},{48,16},{64,96},{80,112},{96,64},{112,80},{1... | collective-permute-start | bytes 786440 | tf_op jit(solution)/shard_map/ppermute | solution.py:49
  216.1 8.1 %collective-permute-start.48 = (bf16[64,1024]{1,0:T(8,128)(2,1)S(1)}, bf16[64,1024]{1,0:T(8,128)(2,1)S(1)}, u32[]{:S(2)}, u32[]{:S(2)}) collective-permute-start(bf16[64,1024]{1,0:T(8,128)(2,1)S(1)} %collective-permute-done.46), channel_id=1, source_target_pairs={{0,1},{1,2},{2,3},{3,4},{4,5},{5,6},{6,7},{7,8},{8,9},{9,10},{10,1... | collective-permute-start | bytes 393224 | tf_op jit(solution)/shard_map/ppermute | solution.py:18
  224.2 9.6 %collective-permute-start.50 = (bf16[64,1024]{1,0:T(8,128)(2,1)S(1)}, bf16[64,1024]{1,0:T(8,128)(2,1)S(1)}, u32[]{:S(2)}, u32[]{:S(2)}) collective-permute-start(bf16[64,1024]{1,0:T(8,128)(2,1)S(1)} %collective-permute-done.48), channel_id=1, source_target_pairs={{0,1},{1,2},{2,3},{3,4},{4,5},{5,6},{6,7},{7,8},{8,9},{9,10},{10,1... | collective-permute-start | bytes 393224 | tf_op jit(solution)/shard_map/ppermute | solution.py:18
  226.1 9.6 %collective-permute-start.51 = (bf16[64,1024]{1,0:T(8,128)(2,1)S(1)}, bf16[64,1024]{1,0:T(8,128)(2,1)S(1)}, u32[]{:S(2)}, u32[]{:S(2)}) collective-permute-start(bf16[64,1024]{1,0:T(8,128)(2,1)S(1)} %collective-permute-done.49), channel_id=1, source_target_pairs={{0,15},{1,0},{2,1},{3,2},{4,3},{5,4},{6,5},{7,6},{8,7},{9,8},{10,9... | collective-permute-start | bytes 393224 | tf_op jit(solution)/shard_map/ppermute | solution.py:21
  231.4 9.5 %collective-permute-start.37 = (f32[2,2,32,256]{3,2,1,0:T(8,128)S(1)}, f32[2,2,32,256]{3,2,1,0:T(8,128)S(1)}, u32[]{:S(2)}, u32[]{:S(2)}) collective-permute-start(f32[2,2,32,256]{3,2,1,0:T(8,128)S(1)} %dynamic-slice_bitcast_fusion.6), channel_id=1, source_target_pairs={{0,128},{16,144},{32,160},{48,176},{64,192},{80,208},{96,224},{112... | collective-permute-start | bytes 393224 | tf_op jit(solution)/shard_map/ppermute | solution.py:49
  233.8 11.2 %collective-permute-start.52 = (bf16[64,1024]{1,0:T(8,128)(2,1)S(1)}, bf16[64,1024]{1,0:T(8,128)(2,1)S(1)}, u32[]{:S(2)}, u32[]{:S(2)}) collective-permute-start(bf16[64,1024]{1,0:T(8,128)(2,1)S(1)} %collective-permute-done.50), channel_id=1, source_target_pairs={{0,1},{1,2},{2,3},{3,4},{4,5},{5,6},{6,7},{7,8},{8,9},{9,10},{10,1... | collective-permute-start | bytes 393224 | tf_op jit(solution)/shard_map/ppermute | solution.py:18
  235.7 18.0 %collective-permute-start.53 = (bf16[64,1024]{1,0:T(8,128)(2,1)S(1)}, bf16[64,1024]{1,0:T(8,128)(2,1)S(1)}, u32[]{:S(2)}, u32[]{:S(2)}) collective-permute-start(bf16[64,1024]{1,0:T(8,128)(2,1)S(1)} %collective-permute-done.51), channel_id=1, source_target_pairs={{0,15},{1,0},{2,1},{3,2},{4,3},{5,4},{6,5},{7,6},{8,7},{9,8},{10,9... | collective-permute-start | bytes 393224 | tf_op jit(solution)/shard_map/ppermute | solution.py:21
  245.0 11.0 %collective-permute-start.54 = (bf16[64,1024]{1,0:T(8,128)(2,1)S(1)}, bf16[64,1024]{1,0:T(8,128)(2,1)S(1)}, u32[]{:S(2)}, u32[]{:S(2)}) collective-permute-start(bf16[64,1024]{1,0:T(8,128)(2,1)S(1)} %collective-permute-done.52), channel_id=1, source_target_pairs={{0,1},{1,2},{2,3},{3,4},{4,5},{5,6},{6,7},{7,8},{8,9},{9,10},{10,1... | collective-permute-start | bytes 393224 | tf_op jit(solution)/shard_map/ppermute | solution.py:18
  256.7 9.8 %collective-permute-start.60 = (bf16[64,1024]{1,0:T(8,128)(2,1)S(1)}, bf16[64,1024]{1,0:T(8,128)(2,1)S(1)}, u32[]{:S(2)}, u32[]{:S(2)}) collective-permute-start(bf16[64,1024]{1,0:T(8,128)(2,1)S(1)} %bitcast.131), channel_id=1, source_target_pairs={{0,1},{1,2},{2,3},{3,4},{4,5},{5,6},{6,7},{7,8},{8,9},{9,10},{10,1... | collective-permute-start | bytes 393224 | tf_op jit(solution)/shard_map/ppermute | solution.py:18
  258.6 9.8 %collective-permute-start.61 = (bf16[64,1024]{1,0:T(8,128)(2,1)S(1)}, bf16[64,1024]{1,0:T(8,128)(2,1)S(1)}, u32[]{:S(2)}, u32[]{:S(2)}) collective-permute-start(bf16[64,1024]{1,0:T(8,128)(2,1)S(1)} %bitcast.132), channel_id=1, source_target_pairs={{0,15},{1,0},{2,1},{3,2},{4,3},{5,4},{6,5},{7,6},{8,7},{9,8},{10,9... | collective-permute-start | bytes 393224 | tf_op jit(solution)/shard_map/ppermute | solution.py:21
  264.3 26.6 %collective-permute-start.55 = (f32[2,2,2,2,32,256]{5,4,2,1,0,3:T(8,128)S(1)}, f32[2,2,2,2,32,256]{5,4,2,1,0,3:T(8,128)S(1)}, u32[]{:S(2)}, u32[]{:S(2)}) collective-permute-start(f32[2,2,2,2,32,256]{5,4,2,1,0,3:T(8,128)S(1)} %bitcast.129), channel_id=1, source_target_pairs={{0,16},{16,0},{32,48},{48,32},{64,80},{80,64},{96,112},{112,96},{1... | collective-permute-start | bytes 1572872 | tf_op jit(solution)/shard_map/ppermute | solution.py:49
  266.6 9.0 %collective-permute-start.62 = (bf16[64,1024]{1,0:T(8,128)(2,1)S(1)}, bf16[64,1024]{1,0:T(8,128)(2,1)S(1)}, u32[]{:S(2)}, u32[]{:S(2)}) collective-permute-start(bf16[64,1024]{1,0:T(8,128)(2,1)S(1)} %collective-permute-done.60), channel_id=1, source_target_pairs={{0,1},{1,2},{2,3},{3,4},{4,5},{5,6},{6,7},{7,8},{8,9},{9,10},{10,1... | collective-permute-start | bytes 393224 | tf_op jit(solution)/shard_map/ppermute | solution.py:18
  268.5 9.0 %collective-permute-start.63 = (bf16[64,1024]{1,0:T(8,128)(2,1)S(1)}, bf16[64,1024]{1,0:T(8,128)(2,1)S(1)}, u32[]{:S(2)}, u32[]{:S(2)}) collective-permute-start(bf16[64,1024]{1,0:T(8,128)(2,1)S(1)} %collective-permute-done.61), channel_id=1, source_target_pairs={{0,15},{1,0},{2,1},{3,2},{4,3},{5,4},{6,5},{7,6},{8,7},{9,8},{10,9... | collective-permute-start | bytes 393224 | tf_op jit(solution)/shard_map/ppermute | solution.py:21
  275.6 8.1 %collective-permute-start.64 = (bf16[64,1024]{1,0:T(8,128)(2,1)S(1)}, bf16[64,1024]{1,0:T(8,128)(2,1)S(1)}, u32[]{:S(2)}, u32[]{:S(2)}) collective-permute-start(bf16[64,1024]{1,0:T(8,128)(2,1)S(1)} %collective-permute-done.62), channel_id=1, source_target_pairs={{0,1},{1,2},{2,3},{3,4},{4,5},{5,6},{6,7},{7,8},{8,9},{9,10},{10,1... | collective-permute-start | bytes 393224 | tf_op jit(solution)/shard_map/ppermute | solution.py:18
  277.5 8.1 %collective-permute-start.65 = (bf16[64,1024]{1,0:T(8,128)(2,1)S(1)}, bf16[64,1024]{1,0:T(8,128)(2,1)S(1)}, u32[]{:S(2)}, u32[]{:S(2)}) collective-permute-start(bf16[64,1024]{1,0:T(8,128)(2,1)S(1)} %collective-permute-done.63), channel_id=1, source_target_pairs={{0,15},{1,0},{2,1},{3,2},{4,3},{5,4},{6,5},{7,6},{8,7},{9,8},{10,9... | collective-permute-start | bytes 393224 | tf_op jit(solution)/shard_map/ppermute | solution.py:21
  283.7 9.2 %collective-permute-start.66 = (bf16[64,1024]{1,0:T(8,128)(2,1)S(1)}, bf16[64,1024]{1,0:T(8,128)(2,1)S(1)}, u32[]{:S(2)}, u32[]{:S(2)}) collective-permute-start(bf16[64,1024]{1,0:T(8,128)(2,1)S(1)} %collective-permute-done.64), channel_id=1, source_target_pairs={{0,1},{1,2},{2,3},{3,4},{4,5},{5,6},{6,7},{7,8},{8,9},{9,10},{10,1... | collective-permute-start | bytes 393224 | tf_op jit(solution)/shard_map/ppermute | solution.py:18
  285.6 9.2 %collective-permute-start.67 = (bf16[64,1024]{1,0:T(8,128)(2,1)S(1)}, bf16[64,1024]{1,0:T(8,128)(2,1)S(1)}, u32[]{:S(2)}, u32[]{:S(2)}) collective-permute-start(bf16[64,1024]{1,0:T(8,128)(2,1)S(1)} %collective-permute-done.65), channel_id=1, source_target_pairs={{0,15},{1,0},{2,1},{3,2},{4,3},{5,4},{6,5},{7,6},{8,7},{9,8},{10,9... | collective-permute-start | bytes 393224 | tf_op jit(solution)/shard_map/ppermute | solution.py:21
  290.9 38.4 %collective-permute-start.56 = (f32[2,2,2,32,256]{4,3,2,1,0:T(8,128)S(1)}, f32[2,2,2,32,256]{4,3,2,1,0:T(8,128)S(1)}, u32[]{:S(2)}, u32[]{:S(2)}) collective-permute-start(f32[2,2,2,32,256]{4,3,2,1,0:T(8,128)S(1)} %dynamic-slice_bitcast_fusion.1), channel_id=1, source_target_pairs={{0,32},{16,48},{32,0},{48,16},{64,96},{80,112},{96,64},{112,80},{1... | collective-permute-start | bytes 786440 | tf_op jit(solution)/shard_map/ppermute | solution.py:49
  292.9 8.1 %collective-permute-start.68 = (bf16[64,1024]{1,0:T(8,128)(2,1)S(1)}, bf16[64,1024]{1,0:T(8,128)(2,1)S(1)}, u32[]{:S(2)}, u32[]{:S(2)}) collective-permute-start(bf16[64,1024]{1,0:T(8,128)(2,1)S(1)} %collective-permute-done.66), channel_id=1, source_target_pairs={{0,1},{1,2},{2,3},{3,4},{4,5},{5,6},{6,7},{7,8},{8,9},{9,10},{10,1... | collective-permute-start | bytes 393224 | tf_op jit(solution)/shard_map/ppermute | solution.py:18
  301.0 8.1 %collective-permute-start.70 = (bf16[64,1024]{1,0:T(8,128)(2,1)S(1)}, bf16[64,1024]{1,0:T(8,128)(2,1)S(1)}, u32[]{:S(2)}, u32[]{:S(2)}) collective-permute-start(bf16[64,1024]{1,0:T(8,128)(2,1)S(1)} %collective-permute-done.68), channel_id=1, source_target_pairs={{0,1},{1,2},{2,3},{3,4},{4,5},{5,6},{6,7},{7,8},{8,9},{9,10},{10,1... | collective-permute-start | bytes 393224 | tf_op jit(solution)/shard_map/ppermute | solution.py:18
  309.0 8.1 %collective-permute-start.72 = (bf16[64,1024]{1,0:T(8,128)(2,1)S(1)}, bf16[64,1024]{1,0:T(8,128)(2,1)S(1)}, u32[]{:S(2)}, u32[]{:S(2)}) collective-permute-start(bf16[64,1024]{1,0:T(8,128)(2,1)S(1)} %collective-permute-done.70), channel_id=1, source_target_pairs={{0,1},{1,2},{2,3},{3,4},{4,5},{5,6},{6,7},{7,8},{8,9},{9,10},{10,1... | collective-permute-start | bytes 393224 | tf_op jit(solution)/shard_map/ppermute | solution.py:18
  333.1 12.5 %collective-permute-start.76 = (f32[2,2,2,40,256]{4,3,2,1,0:T(8,128)S(1)}, f32[2,2,2,40,256]{4,3,2,1,0:T(8,128)S(1)}, u32[]{:S(2)}, u32[]{:S(2)}) collective-permute-start(f32[2,2,2,40,256]{4,3,2,1,0:T(8,128)S(1)} %dynamic-slice_bitcast_fusion), channel_id=1, source_target_pairs={{0,32},{16,48},{32,0},{48,16},{64,96},{80,112},{96,64},{112,80},{1... | collective-permute-start | bytes 983048 | tf_op jit(solution)/shard_map/ppermute | solution.py:49
  337.3 11.0 %collective-permute-start.58 = (f32[2,32,256]{2,1,0:T(8,128)S(1)}, f32[2,32,256]{2,1,0:T(8,128)S(1)}, u32[]{:S(2)}, u32[]{:S(2)}) collective-permute-start(f32[2,32,256]{2,1,0:T(8,128)S(1)} %dynamic-slice_bitcast_fusion.9), channel_id=1, source_target_pairs={{0,64},{16,80},{32,96},{48,112},{64,0},{80,16},{96,32},{112,48},{1... | collective-permute-start | bytes 196616 | tf_op jit(solution)/shard_map/ppermute | solution.py:49
  352.9 10.2 %collective-permute-start.78 = (f32[2,40,256]{2,1,0:T(8,128)S(1)}, f32[2,40,256]{2,1,0:T(8,128)S(1)}, u32[]{:S(2)}, u32[]{:S(2)}) collective-permute-start(f32[2,40,256]{2,1,0:T(8,128)S(1)} %dynamic-slice_bitcast_fusion.8), channel_id=1, source_target_pairs={{0,64},{16,80},{32,96},{48,112},{64,0},{80,16},{96,32},{112,48},{1... | collective-permute-start | bytes 245768 | tf_op jit(solution)/shard_map/ppermute | solution.py:49
  (22 other events, 212.2 us)
